TPU v7x, 256 devices: a whole 4x4x8 slice. The times are simulated.
256 devices in a mesh: seq: 16 (over z_lo, y), grp: 16 (over x, z_hi, core).
Axes of the slice: x: 4, y: 4, z: 8 (z_hi: 2, z_lo: 4; z = z_hi * 4 + z_lo), core: 2. Of those that a mesh axis runs over, the one named last changes fastest.
Arguments:
- pre_x: bfloat16 [8192, 16384], P('seq', 'grp'), may hold values from -6 to 6
- pre_b: bfloat16 [8192, 2048], P('seq'), may hold values from -6 to 6
- pre_c: bfloat16 [8192, 2048], P('seq'), may hold values from -6 to 6
- pre_dt: float32 [256, 8192], P('grp', 'seq'), may hold values from 0.004 to 0.016
- decay_rate: float32 [256], replicated, may hold values from 0.00390625 to 5
- skip_gain: float32 [256], replicated, may hold values from 0.5 to 1.5
- conv_taps: float32 [4, 20480], replicated, may hold values from -3 to 3
- dec_x: bfloat16 [2, 128, 16384], P(None, 'grp', 'seq'), may hold values from -6 to 6
- dec_b: bfloat16 [2, 128, 2048], P(None, 'grp'), may hold values from -6 to 6
- dec_c: bfloat16 [2, 128, 2048], P(None, 'grp'), may hold values from -6 to 6
- dec_dt: float32 [2, 128, 256], P(None, 'grp', 'seq'), may hold values from 0.004 to 0.016
- dec_query: bfloat16 [2, 128, 8192], P(None, 'grp'), may hold values from -12 to 12
- new_kv: bfloat16 [2, 2, 128, 1024], P(None, None, 'grp'), may hold values from -6 to 6
- cache_kv: bfloat16 [2, 128, 1024, 1024], P(None, 'grp', 'seq'), may hold values from -12 to 12
- kv_len: int32 [128], P('grp'), may hold values from 2 to 1024, as said below
Outputs:
- pre_y: bfloat16 [8192, 16384], P('seq', 'grp')
- dec_y: bfloat16 [2, 128, 16384], P(None, 'grp', 'seq')
- attn_out: bfloat16 [2, 128, 8192], P(None, 'grp', 'seq')
Inputs may be any that keep to these rules, and one draw needn't show every extreme that they name: `kv_len`: row 0 of every group of 8 rows has all 1024 positions valid.
All inputs are finite; a program needn't handle non-finite values.
Results may differ from a plain program's by a relative error of at most 0.0013.
Values sent between devices are 32-bit elements; how exact they have to be, the bound alone decides.
No kernel may reach another device: no remote copies, remote signals or barrier semaphores. Data moves between devices by JAX's collectives and lax.ppermute only.
A program may use at most 128 MiB of HBM per device.

v0:
```python
import jax
import jax.numpy as jnp
from jax import lax
from jax.sharding import PartitionSpec as P

HEADS = 256
HDIM = 64
STATE = 256
GROUPS = 8
TAPS = 4
QHEADS = 64
KVHEADS = 8
ADIM = 128
SPAN = 256
STEPS = 2


HIGH = lax.Precision.HIGHEST
NEG = -1e30


def passed_along(value, axis, steps):
    count = lax.axis_size(axis)
    first, last = (max(0, -steps), min(count, count - steps))
    return lax.ppermute(value, axis, [(source, source + steps) for source in range(first, last)])


def from_root(value, axis, source):
    kept = jnp.where(lax.axis_index(axis) == source, value, 0).astype(value.dtype)
    return lax.psum(kept, axis)


def joined(value, axis, join):
    pieces = jax.tree.map(lambda part: lax.all_gather(part, axis), value)
    head = jax.tree.map(lambda part: part[0], pieces)
    tail = jax.tree.map(lambda part: part[1:], pieces)
    subtotal, _ = lax.scan(lambda subtotal, share: (join(subtotal, share), None), head, tail)
    return subtotal


def causal_conv(leading, source, kernel):
    row_total = source.shape[0]
    padded = jnp.concatenate([leading, source], axis=0)
    accumulated = jnp.zeros_like(source)
    for position in range(TAPS):
        accumulated = accumulated + kernel[position] * padded[position : position + row_total]
    return jax.nn.silu(accumulated)


def decode_conv(leading, fresh, kernel):
    results = []
    for current in range(fresh.shape[0]):
        accumulated = jnp.zeros(fresh.shape[1:], jnp.float32)
        for position in range(TAPS):
            place = current + position
            if place < TAPS - 1:
                term = leading[place][None, :]
            else:
                term = fresh[place - (TAPS - 1)]
            accumulated = accumulated + kernel[position] * term
        results.append(jax.nn.silu(accumulated))
    return jnp.stack(results)


def span_pass(ssm_state, block):
    inputs, entries, readout, log_decay = block
    cumulative = jnp.cumsum(log_decay, axis=1)
    block_size = log_decay.shape[1]
    causal = jnp.arange(block_size)[:, None] >= jnp.arange(block_size)[None, :]
    spreads = cumulative[:, :, None] - cumulative[:, None, :]
    weights = jnp.where(causal[None], jnp.exp(jnp.where(causal[None], spreads, 0.0)), 0.0)
    intersection = jnp.dot(readout, entries.T, precision=HIGH)
    intra_span = jnp.einsum("kts,skp->tkp", weights * intersection[None], inputs, precision=HIGH)
    carried = jnp.exp(cumulative).T[:, :, None] * jnp.einsum(
        "tn,kpn->tkp", readout, ssm_state, precision=HIGH
    )
    remaining = jnp.exp(cumulative[:, -1:] - cumulative)
    updates = jnp.einsum("skp,sn->kpn", inputs * remaining.T[:, :, None], entries, precision=HIGH)
    renewed = jnp.exp(cumulative[:, -1])[:, None, None] * ssm_state + updates
    return (renewed, intra_span + carried)


def run_spans(inputs, entries, readout, log_decay, ssm_state):
    row_total, heads_here, head_width = inputs.shape
    block_total = row_total // SPAN
    blocks = (
        inputs.reshape(block_total, SPAN, heads_here, head_width),
        entries.reshape(block_total, SPAN, entries.shape[1]),
        readout.reshape(block_total, SPAN, readout.shape[1]),
        log_decay.reshape(heads_here, block_total, SPAN).transpose(1, 0, 2),
    )
    ssm_state, results = lax.scan(span_pass, ssm_state, blocks)
    return (results.reshape(row_total, heads_here, head_width), ssm_state)


def decode_mamba(ssm_state, heads_x, heads_b, heads_c, step_dt, rates, gains):
    decays = jnp.exp(-step_dt * rates)
    from_prefix = jnp.einsum("jrhn,hpn->jrhp", heads_c, ssm_state, precision=HIGH)
    results = []
    for current in range(heads_x.shape[0]):
        factor = jnp.ones(decays.shape[1:], jnp.float32)
        accumulated = gains[None, :, None] * heads_x[current]
        for earlier in range(current, -1, -1):
            intersection = jnp.sum(heads_c[current] * heads_b[earlier], axis=-1)
            accumulated = (
                accumulated
                + (factor * step_dt[earlier] * intersection)[..., None] * heads_x[earlier]
            )
            factor = factor * decays[earlier]
        accumulated = accumulated + factor[..., None] * from_prefix[current]
        results.append(accumulated)
    return jnp.stack(results)


def group_layout(head_begin, head_count):
    per_group = HEADS // GROUPS
    group_count = max(1, head_count // per_group)
    return (head_begin // per_group, group_count, head_count // group_count)


def fold_partial(former, latter):
    peak_score = jnp.maximum(former[0], latter[0])
    former_scale = jnp.exp(former[0] - peak_score)
    latter_scale = jnp.exp(latter[0] - peak_score)
    weight_sum = former[1] * former_scale + latter[1] * latter_scale
    summed = former[2] * former_scale[..., None] + latter[2] * latter_scale[..., None]
    return (peak_score, weight_sum, summed)


def on_device(
    pre_x,
    pre_b,
    pre_c,
    pre_dt,
    decay_rate,
    skip_gain,
    conv_taps,
    dec_x,
    dec_b,
    dec_c,
    dec_dt,
    dec_query,
    new_kv,
    cache_kv,
    kv_len,
):
    seq_count = lax.axis_size("seq")
    seq_index = lax.axis_index("seq")
    grp_index = lax.axis_index("grp")
    section = pre_x.shape[0]
    local_heads = pre_x.shape[1] // HDIM
    edge = TAPS - 1
    x_offset = HEADS * HDIM
    c_offset = HEADS * HDIM + GROUPS * STATE
    head_begin = grp_index * local_heads
    group_begin, group_count, heads_each = group_layout(head_begin, local_heads)
    source_x = pre_x.astype(jnp.float32)
    full_b = pre_b.astype(jnp.float32)
    full_c = pre_c.astype(jnp.float32)
    tail_rows = (source_x[section - edge :], full_b[section - edge :], full_c[section - edge :])
    leading = passed_along((tail_rows[0], tail_rows[1], tail_rows[2]), "seq", 1)
    kernel_x = lax.dynamic_slice_in_dim(conv_taps, head_begin * HDIM, local_heads * HDIM, 1)
    kernel_b = lax.dynamic_slice_in_dim(
        conv_taps, x_offset + group_begin * STATE, group_count * STATE, 1
    )
    kernel_c = lax.dynamic_slice_in_dim(
        conv_taps, c_offset + group_begin * STATE, group_count * STATE, 1
    )
    conv_x = causal_conv(leading[0], source_x, kernel_x)
    conv_b = causal_conv(
        lax.dynamic_slice_in_dim(leading[1], group_begin * STATE, group_count * STATE, 1),
        lax.dynamic_slice_in_dim(full_b, group_begin * STATE, group_count * STATE, 1),
        kernel_b,
    )
    conv_c = causal_conv(
        lax.dynamic_slice_in_dim(leading[2], group_begin * STATE, group_count * STATE, 1),
        lax.dynamic_slice_in_dim(full_c, group_begin * STATE, group_count * STATE, 1),
        kernel_c,
    )
    rates = lax.dynamic_slice_in_dim(decay_rate, head_begin, local_heads, 0)
    gains = lax.dynamic_slice_in_dim(skip_gain, head_begin, local_heads, 0)
    log_decay = -pre_dt * rates[:, None]
    head_inputs = conv_x.reshape(section, local_heads, HDIM)
    scaled = head_inputs * pre_dt.T[:, :, None]
    grouped = scaled.reshape(section, group_count, heads_each, HDIM).transpose(1, 0, 2, 3)
    entries = conv_b.reshape(section, group_count, STATE).transpose(1, 0, 2)
    readout = conv_c.reshape(section, group_count, STATE).transpose(1, 0, 2)
    decay_groups = log_decay.reshape(group_count, heads_each, section)
    blank = jnp.zeros((group_count, heads_each, HDIM, STATE), jnp.float32)
    intra_part, closing_local = jax.vmap(run_spans)(grouped, entries, readout, decay_groups, blank)
    local_state = closing_local.reshape(local_heads, HDIM, STATE)
    cumulative = jnp.cumsum(log_decay, axis=1)
    section_decay = cumulative[:, -1]

    def relay(counter, arriving):
        leaving = jnp.exp(section_decay)[:, None, None] * arriving + local_state
        return passed_along(leaving, "seq", 1)

    incoming = lax.fori_loop(0, seq_count - 1, relay, jnp.zeros_like(local_state))
    incoming_groups = incoming.reshape(group_count, heads_each, HDIM, STATE)
    from_before = jnp.einsum("gsn,gkpn->gskp", readout, incoming_groups, precision=HIGH)
    decay_factor = jnp.exp(cumulative).reshape(group_count, heads_each, section).transpose(0, 2, 1)
    combined = intra_part + decay_factor[..., None] * from_before
    combined = (
        combined.transpose(1, 0, 2, 3).reshape(section, local_heads, HDIM)
        + gains[None, :, None] * head_inputs
    )
    pre_y = combined.reshape(section, local_heads * HDIM).astype(jnp.bfloat16)
    closing = jnp.exp(section_decay)[:, None, None] * incoming + local_state
    final_state, tail_x, tail_b, tail_c = (
        from_root(closing, "seq", seq_count - 1),
        from_root(tail_rows[0], "seq", seq_count - 1),
        from_root(tail_rows[1], "seq", seq_count - 1),
        from_root(tail_rows[2], "seq", seq_count - 1),
    )
    state_heads = HEADS // seq_count
    root_group = seq_index * state_heads // local_heads
    prefix_state, prefix_tail = (
        from_root(final_state, "grp", root_group),
        from_root(tail_x, "grp", root_group),
    )
    rows_here = dec_x.shape[1]
    dec_begin = seq_index * state_heads
    dgroup_begin, dgroup_count, dheads_each = group_layout(dec_begin, state_heads)
    kernel_dx = lax.dynamic_slice_in_dim(conv_taps, dec_begin * HDIM, state_heads * HDIM, 1)
    kernel_db = lax.dynamic_slice_in_dim(
        conv_taps, x_offset + dgroup_begin * STATE, dgroup_count * STATE, 1
    )
    kernel_dc = lax.dynamic_slice_in_dim(
        conv_taps, c_offset + dgroup_begin * STATE, dgroup_count * STATE, 1
    )
    step_x = decode_conv(prefix_tail, dec_x.astype(jnp.float32), kernel_dx)
    step_b = decode_conv(
        lax.dynamic_slice_in_dim(tail_b, dgroup_begin * STATE, dgroup_count * STATE, 1),
        lax.dynamic_slice_in_dim(dec_b, dgroup_begin * STATE, dgroup_count * STATE, 2).astype(
            jnp.float32
        ),
        kernel_db,
    )
    step_c = decode_conv(
        lax.dynamic_slice_in_dim(tail_c, dgroup_begin * STATE, dgroup_count * STATE, 1),
        lax.dynamic_slice_in_dim(dec_c, dgroup_begin * STATE, dgroup_count * STATE, 2).astype(
            jnp.float32
        ),
        kernel_dc,
    )
    heads_x = step_x.reshape(STEPS, rows_here, state_heads, HDIM)
    heads_b = jnp.repeat(step_b.reshape(STEPS, rows_here, dgroup_count, STATE), dheads_each, axis=2)
    heads_c = jnp.repeat(step_c.reshape(STEPS, rows_here, dgroup_count, STATE), dheads_each, axis=2)
    dec_rates = lax.dynamic_slice_in_dim(decay_rate, dec_begin, state_heads, 0)
    dec_gains = lax.dynamic_slice_in_dim(skip_gain, dec_begin, state_heads, 0)
    mamba_out = decode_mamba(prefix_state, heads_x, heads_b, heads_c, dec_dt, dec_rates, dec_gains)
    dec_y = mamba_out.reshape(STEPS, rows_here, state_heads * HDIM).astype(jnp.bfloat16)
    group_size = QHEADS // KVHEADS
    score_scale = ADIM ** (-0.5)
    positions = cache_kv.shape[2]
    queries = dec_query.reshape(STEPS, rows_here, KVHEADS, group_size, ADIM)
    key_rows = cache_kv[0].reshape(rows_here, positions, KVHEADS, ADIM)
    value_rows = cache_kv[1].reshape(rows_here, positions, KVHEADS, ADIM).astype(jnp.float32)
    scores = (
        jnp.einsum("jrkgd,rckd->jrkgc", queries, key_rows, preferred_element_type=jnp.float32)
        * score_scale
    )
    places = seq_index * positions + jnp.arange(positions)
    usable = (places[None, :] < kv_len[:, None])[None, :, None, None, :]
    scores = jnp.where(usable, scores, NEG)
    peak_local = jnp.max(scores, axis=-1)
    weights = jnp.where(usable, jnp.exp(scores - peak_local[..., None]), 0.0)
    mass_local = jnp.sum(weights, axis=-1)
    summed_local = jnp.einsum("jrkgc,rckd->jrkgd", weights, value_rows, precision=HIGH)
    peak_local = peak_local.reshape(STEPS, rows_here, QHEADS)
    mass_local = mass_local.reshape(STEPS, rows_here, QHEADS)
    summed_local = summed_local.reshape(STEPS, rows_here, QHEADS, ADIM)
    own_heads = QHEADS // seq_count
    head_start = seq_index * own_heads
    merged = joined((peak_local, mass_local, summed_local), "seq", fold_partial)
    peak_cache = lax.dynamic_slice_in_dim(merged[0], head_start, own_heads, 2)
    mass_cache = lax.dynamic_slice_in_dim(merged[1], head_start, own_heads, 2)
    summed_cache = lax.dynamic_slice_in_dim(merged[2], head_start, own_heads, 2)
    new_keys = new_kv[0].reshape(STEPS, rows_here, KVHEADS, ADIM)
    new_values = new_kv[1].reshape(STEPS, rows_here, KVHEADS, ADIM).astype(jnp.float32)
    new_scores = (
        jnp.einsum("jrkgd,irkd->jrkgi", queries, new_keys, preferred_element_type=jnp.float32)
        * score_scale
    )
    allowed = (jnp.arange(STEPS)[None, :] <= jnp.arange(STEPS)[:, None])[:, None, None, None, :]
    new_scores = jnp.where(allowed, new_scores, NEG)
    new_scores = lax.dynamic_slice_in_dim(
        new_scores.reshape(STEPS, rows_here, QHEADS, STEPS), head_start, own_heads, 2
    )
    allowed_heads = (jnp.arange(STEPS)[None, :] <= jnp.arange(STEPS)[:, None])[:, None, None, :]
    head_kv = (head_start + jnp.arange(own_heads)) // group_size
    pick = (head_kv[:, None] == jnp.arange(KVHEADS)[None, :]).astype(jnp.float32)
    own_values = jnp.einsum("hk,irkd->irhd", pick, new_values, precision=HIGH)
    peak_total = jnp.maximum(peak_cache, jnp.max(new_scores, axis=-1))
    cache_scale = jnp.exp(peak_cache - peak_total)
    new_weights = jnp.where(allowed_heads, jnp.exp(new_scores - peak_total[..., None]), 0.0)
    mass_total = mass_cache * cache_scale + jnp.sum(new_weights, axis=-1)
    summed_total = summed_cache * cache_scale[..., None] + jnp.einsum(
        "jrhi,irhd->jrhd", new_weights, own_values, precision=HIGH
    )
    attn_out = (
        (summed_total / mass_total[..., None])
        .reshape(STEPS, rows_here, own_heads * ADIM)
        .astype(jnp.bfloat16)
    )
    return (pre_y, dec_y, attn_out)


def solution(mesh):
    in_specs = (
        P("seq", "grp"),
        P("seq", None),
        P("seq", None),
        P("grp", "seq"),
        P(),
        P(),
        P(),
        P(None, "grp", "seq"),
        P(None, "grp", None),
        P(None, "grp", None),
        P(None, "grp", "seq"),
        P(None, "grp", None),
        P(None, None, "grp", None),
        P(None, "grp", "seq", None),
        P("grp"),
    )
    out_specs = (P("seq", "grp"), P(None, "grp", "seq"), P(None, "grp", "seq"))
    return jax.shard_map(
        on_device, mesh=mesh, in_specs=in_specs, out_specs=out_specs, check_vma=False
    )
```

profile of v0, /device:TPU:8, one launch (start us, length us, event | category | flops | bytes accessed | tf_op | source)
XLA Modules:
  0.0 1164.7 jit_solution(2803646469670507166)
XLA Ops:
  33.9 72.7 %all-reduce = (f32[3,2048]{1,0:T(4,128)}, f32[3,2048]{1,0:T(4,128)}, f32[3,1024]{1,0:T(4,128)}) all-reduce(f32[3,2048]{1,0:T(4,128)S(1)} %broadcast_select_fusion.2, f32[3,2048]{1,0:T(4,128)S(1)} %broadcast_select_fusion.1, f32[3,1024]{1,0:T(4,128)S(1)} %broadcast_select_fusion.4), channel_id=1, replica_groups=mesh['seq'=16,'grp'=16] {'seq'}, use_global_device_ids=true, to_apply=%region_10.11 | all-reduce | flops 15360 | bytes 122880 | tf_op jit(solution)/shard_map/psum | solution.py:30
  106.5 85.8 %psum.43 = f32[3,1024]{1,0:T(4,128)S(1)} all-reduce(f32[3,1024]{1,0:T(4,128)S(1)} %broadcast_select_fusion.3), channel_id=1, replica_groups=mesh['seq'=16,'grp'=16] {'grp'}, use_global_device_ids=true, to_apply=%region_9.10 | all-reduce | flops 3072 | bytes 24576 | tf_op jit(solution)/shard_map/psum | solution.py:30
  217.9 73.1 %while.41 = (s32[]{:T(128)}, f32[1,16,64,256]{3,2,1,0:T(8,128)S(1)}, f32[2,1,256,16,64]{2,0,4,3,1:T(2,128)}, f32[2,1,16,256]{3,0,2,1:T(2,128)S(1)}, f32[2,1,256,...) while((s32[]{:T(128)}, ...), condition=%wide.region_3.4_spmd.clone, body=%wide.region_0.3_spmd.clone.sunk | while | flops 2623873024 | bytes 25218784 | solution.py:92
  229.6 21.9 %dynamic_update_slice.6 = f32[2,1,256,16,64]{2,0,4,3,1:T(2,128)} dynamic-update-slice(f32[2,1,256,16,64]{2,0,4,3,1:T(2,128)} %get-tuple-element.428, f32[1,1,256,16,64]{2,0,4,3,1:T(1,128)S(1)} %copy.283, s32[]{:T(128)} %get-tuple-element.426, s32[]{:T(128)} %constant.121.clone.1..sunk, s32[]{:T(128)} %constant.121.clone.1..sunk, s32[]{:T(128)} %constant.121.clone.1..sunk, s32[]{:T(128)} %constant.121.clone.1..sunk) | dynamic-update-slice | bytes 2097156 | tf_op jit(solution)/shard_map/vmap()/while/body/jit(dynamic_update_index_in_dim)/dynamic_update_slice | solution.py:92
  266.2 21.9 %dynamic_update_slice.6 = f32[2,1,256,16,64]{2,0,4,3,1:T(2,128)} dynamic-update-slice(f32[2,1,256,16,64]{2,0,4,3,1:T(2,128)} %get-tuple-element.428, f32[1,1,256,16,64]{2,0,4,3,1:T(1,128)S(1)} %copy.283, s32[]{:T(128)} %get-tuple-element.426, s32[]{:T(128)} %constant.121.clone.1..sunk, s32[]{:T(128)} %constant.121.clone.1..sunk, s32[]{:T(128)} %constant.121.clone.1..sunk, s32[]{:T(128)} %constant.121.clone.1..sunk) | dynamic-update-slice | bytes 2097156 | tf_op jit(solution)/shard_map/vmap()/while/body/jit(dynamic_update_index_in_dim)/dynamic_update_slice | solution.py:92
  291.1 375.0 %while.39 = (s32[]{:T(128)}, f32[16,64,256]{2,1,0:T(8,128)S(1)}, f32[16,1,1]{0,2,1:T(1,128)S(1)}, f32[16,64,256]{2,1,0:T(8,128)S(1)}, s32[]{:T(128)}) while((s32[]{:T(128)}, f32[16,64,256]{2,1,0:T(8,128)S(1)}, f32[16,1,1]{0,2,1:T(1,128)S(1)}, f32[16,64,256]{2,1,0:T(8,128)S(1)}, s32[]{:T(128)}) %tuple.133), condition=%wide.region_7.8_spmd, body=%wide.region_6.7_spmd.sunk | while | flops 524290 | bytes 7340197 | solution.py:199
  293.3 22.6 %collective-permute-done = f32[16,64,256]{2,1,0:T(8,128)S(1)} collective-permute-done((f32[16,64,256]{2,1,0:T(8,128)S(1)}, f32[16,64,256]{2,1,0:T(8,128)S(1)}, u32[]{:S(2)}, u32[]{:S(2)}) %collective-permute-start) | collective-permute-done | bytes 1048608 | tf_op jit(solution)/shard_map/while/body/eval_jaxpr/ppermute | solution.py:25
  318.1 21.2 %collective-permute-done = f32[16,64,256]{2,1,0:T(8,128)S(1)} collective-permute-done((f32[16,64,256]{2,1,0:T(8,128)S(1)}, f32[16,64,256]{2,1,0:T(8,128)S(1)}, u32[]{:S(2)}, u32[]{:S(2)}) %collective-permute-start) | collective-permute-done | bytes 1048608 | tf_op jit(solution)/shard_map/while/body/eval_jaxpr/ppermute | solution.py:25
  341.4 21.2 %collective-permute-done = f32[16,64,256]{2,1,0:T(8,128)S(1)} collective-permute-done((f32[16,64,256]{2,1,0:T(8,128)S(1)}, f32[16,64,256]{2,1,0:T(8,128)S(1)}, u32[]{:S(2)}, u32[]{:S(2)}) %collective-permute-start) | collective-permute-done | bytes 1048608 | tf_op jit(solution)/shard_map/while/body/eval_jaxpr/ppermute | solution.py:25
  364.7 21.2 %collective-permute-done = f32[16,64,256]{2,1,0:T(8,128)S(1)} collective-permute-done((f32[16,64,256]{2,1,0:T(8,128)S(1)}, f32[16,64,256]{2,1,0:T(8,128)S(1)}, u32[]{:S(2)}, u32[]{:S(2)}) %collective-permute-start) | collective-permute-done | bytes 1048608 | tf_op jit(solution)/shard_map/while/body/eval_jaxpr/ppermute | solution.py:25
  388.0 22.3 %collective-permute-done = f32[16,64,256]{2,1,0:T(8,128)S(1)} collective-permute-done((f32[16,64,256]{2,1,0:T(8,128)S(1)}, f32[16,64,256]{2,1,0:T(8,128)S(1)}, u32[]{:S(2)}, u32[]{:S(2)}) %collective-permute-start) | collective-permute-done | bytes 1048608 | tf_op jit(solution)/shard_map/while/body/eval_jaxpr/ppermute | solution.py:25
  412.4 23.4 %collective-permute-done = f32[16,64,256]{2,1,0:T(8,128)S(1)} collective-permute-done((f32[16,64,256]{2,1,0:T(8,128)S(1)}, f32[16,64,256]{2,1,0:T(8,128)S(1)}, u32[]{:S(2)}, u32[]{:S(2)}) %collective-permute-start) | collective-permute-done | bytes 1048608 | tf_op jit(solution)/shard_map/while/body/eval_jaxpr/ppermute | solution.py:25
  437.9 24.6 %collective-permute-done = f32[16,64,256]{2,1,0:T(8,128)S(1)} collective-permute-done((f32[16,64,256]{2,1,0:T(8,128)S(1)}, f32[16,64,256]{2,1,0:T(8,128)S(1)}, u32[]{:S(2)}, u32[]{:S(2)}) %collective-permute-start) | collective-permute-done | bytes 1048608 | tf_op jit(solution)/shard_map/while/body/eval_jaxpr/ppermute | solution.py:25
  464.6 25.7 %collective-permute-done = f32[16,64,256]{2,1,0:T(8,128)S(1)} collective-permute-done((f32[16,64,256]{2,1,0:T(8,128)S(1)}, f32[16,64,256]{2,1,0:T(8,128)S(1)}, u32[]{:S(2)}, u32[]{:S(2)}) %collective-permute-start) | collective-permute-done | bytes 1048608 | tf_op jit(solution)/shard_map/while/body/eval_jaxpr/ppermute | solution.py:25
  492.4 25.1 %collective-permute-done = f32[16,64,256]{2,1,0:T(8,128)S(1)} collective-permute-done((f32[16,64,256]{2,1,0:T(8,128)S(1)}, f32[16,64,256]{2,1,0:T(8,128)S(1)}, u32[]{:S(2)}, u32[]{:S(2)}) %collective-permute-start) | collective-permute-done | bytes 1048608 | tf_op jit(solution)/shard_map/while/body/eval_jaxpr/ppermute | solution.py:25
  520.0 24.0 %collective-permute-done = f32[16,64,256]{2,1,0:T(8,128)S(1)} collective-permute-done((f32[16,64,256]{2,1,0:T(8,128)S(1)}, f32[16,64,256]{2,1,0:T(8,128)S(1)}, u32[]{:S(2)}, u32[]{:S(2)}) %collective-permute-start) | collective-permute-done | bytes 1048608 | tf_op jit(solution)/shard_map/while/body/eval_jaxpr/ppermute | solution.py:25
  546.6 22.9 %collective-permute-done = f32[16,64,256]{2,1,0:T(8,128)S(1)} collective-permute-done((f32[16,64,256]{2,1,0:T(8,128)S(1)}, f32[16,64,256]{2,1,0:T(8,128)S(1)}, u32[]{:S(2)}, u32[]{:S(2)}) %collective-permute-start) | collective-permute-done | bytes 1048608 | tf_op jit(solution)/shard_map/while/body/eval_jaxpr/ppermute | solution.py:25
  572.4 21.7 %collective-permute-done = f32[16,64,256]{2,1,0:T(8,128)S(1)} collective-permute-done((f32[16,64,256]{2,1,0:T(8,128)S(1)}, f32[16,64,256]{2,1,0:T(8,128)S(1)}, u32[]{:S(2)}, u32[]{:S(2)}) %collective-permute-start) | collective-permute-done | bytes 1048608 | tf_op jit(solution)/shard_map/while/body/eval_jaxpr/ppermute | solution.py:25
  669.7 167.4 %all-reduce.4.cloned.1.call-done = f32[16,64,256]{2,1,0:T(8,128)} async-done(((f32[16,64,256]{2,1,0:T(8,128)}), f32[16,64,256]{2,1,0:T(8,128)}) %all-reduce.4.cloned.1.call-update) | async-done | bytes 1048592 | tf_op jit(solution)/shard_map/psum | solution.py:30
  843.1 39.8 %all_gather.10 = f32[16,2,8,64]{3,2,1,0:T(8,128)S(1)} all-gather(f32[1,2,8,64]{3,2,1,0:T(8,128)S(1)} %all_gather_reshape.10), channel_id=1, replica_groups=mesh['seq'=16,'grp'=16] {'seq'}, dimensions={0}, use_global_device_ids=true | all-gather | bytes 69632 | tf_op jit(solution)/shard_map/all_gather | solution.py:34
  883.0 41.6 %all_gather.9 = f32[16,2,8,64]{3,2,1,0:T(8,128)S(1)} all-gather(f32[1,2,8,64]{3,2,1,0:T(8,128)S(1)} %all_gather_reshape.9), channel_id=1, replica_groups=mesh['seq'=16,'grp'=16] {'seq'}, dimensions={0}, use_global_device_ids=true | all-gather | bytes 69632 | tf_op jit(solution)/shard_map/all_gather | solution.py:34
  952.7 67.6 %all-reduce.6.cloned.1.call-done = f32[16,64,256]{2,1,0:T(8,128)} async-done(((f32[16,64,256]{2,1,0:T(8,128)}), f32[16,64,256]{2,1,0:T(8,128)}) %all-reduce.6.cloned.1.call-update) | async-done | bytes 1048592 | tf_op jit(solution)/shard_map/psum | solution.py:30
  1023.7 99.5 %all-gather.2.cloned.1.call-done = f32[16,2,8,64,128]{4,3,2,1,0:T(8,128)} async-done(((f32[1,2,8,64,128]{4,3,2,1,0:T(8,128)}), f32[16,2,8,64,128]{4,3,2,1,0:T(8,128)}) %all-gather.2.cloned.1.call-update) | async-done | bytes 8388624 | tf_op jit(solution)/shard_map/all_gather | solution.py:34
  1132.1 23.9 %while.40 = (s32[]{:T(128)}, f32[2,8,64]{2,1,0:T(8,128)S(1)}, f32[2,8,64]{2,1,0:T(8,128)S(1)}, f32[2,8,64,128]{3,2,1,0:T(8,128)S(1)}, f32[15,2,8,64]{3,2,1,0:T(8...) while((s32[]{:T(128)}, f32[2,8,64]{2,1,0:T(8,128)S(1)}, ...), condition=%wide.region_20.21_spmd, body=%wide.region_19.20_spmd.sunk | while | flops 399362 | bytes 1613917 | solution.py:37
  (340 shorter events, 254.8 us)
Async XLA Ops:
  7.2 831.5 %copy-start = (bf16[2,8,8192]{2,1,0:T(8,128)(2,1)S(1)}, bf16[2,8,8192]{2,1,0:T(8,128)(2,1)}, u32[]{:S(2)}) copy-start(bf16[2,8,8192]{2,1,0:T(8,128)(2,1)} %param.32) | copy-start | bytes 786436
  7.2 830.0 %all-reduce.4.cloned.1.call-start = ((), (), s32[]{:S(2)}) async-start(), calls=%async_computation | async-start | bytes 2097152 | tf_op jit(solution)/shard_map/psum | solution.py:30
  8.6 206.3 %collective-permute-start.2 = (f32[3,2048]{1,0:T(4,128)}, f32[3,2048]{1,0:T(4,128)}, u32[]{:S(2)}, u32[]{:S(2)}) collective-permute-start(f32[3,2048]{1,0:T(4,128)} %slice.340), channel_id=1, source_target_pairs={{0,16},{16,32},{32,48},{48,64},{64,80},{80,96},{96,112},{112,128},... | collective-permute-start | bytes 73736 | tf_op jit(solution)/shard_map/ppermute | solution.py:25
  13.5 201.4 %collective-permute-start.3 = (f32[3,2048]{1,0:T(4,128)}, f32[3,2048]{1,0:T(4,128)}, u32[]{:S(2)}, u32[]{:S(2)}) collective-permute-start(f32[3,2048]{1,0:T(4,128)} %slice.345), channel_id=1, source_target_pairs={{0,16},{16,32},{32,48},{48,64},{64,80},{80,96},{96,112},{112,128},... | collective-permute-start | bytes 73736 | tf_op jit(solution)/shard_map/ppermute | solution.py:25
  18.0 180.5 %collective-permute-start.1 = (f32[3,1024]{1,0:T(4,128)}, f32[3,1024]{1,0:T(4,128)}, u32[]{:S(2)}, u32[]{:S(2)}) collective-permute-start(f32[3,1024]{1,0:T(4,128)} %slice.335), channel_id=1, source_target_pairs={{0,16},{16,32},{32,48},{48,64},{64,80},{80,96},{96,112},{112,128},... | collective-permute-start | bytes 36872 | tf_op jit(solution)/shard_map/ppermute | solution.py:25
  28.5 169.9 %copy-start.3 = (f32[512,1024]{1,0:T(8,128)}, f32[512,1024]{1,0:T(8,128)S(1)}, u32[]{:S(2)}) copy-start(f32[512,1024]{1,0:T(8,128)S(1)} %convert_element_type.40) | copy-start | bytes 6291460
  291.3 24.6 %collective-permute-start = (f32[16,64,256]{2,1,0:T(8,128)S(1)}, f32[16,64,256]{2,1,0:T(8,128)S(1)}, u32[]{:S(2)}, u32[]{:S(2)}) collective-permute-start(f32[16,64,256]{2,1,0:T(8,128)S(1)} %multiply_add_fusion.7), channel_id=1, source_target_pairs={{0,16},{16,32},{32,48},{48,64},{64,80},{80,96},{96,112},{112,128},... | collective-permute-start | bytes 3145736 | tf_op jit(solution)/shard_map/while/body/eval_jaxpr/ppermute | solution.py:25
  316.1 23.1 %collective-permute-start = (f32[16,64,256]{2,1,0:T(8,128)S(1)}, f32[16,64,256]{2,1,0:T(8,128)S(1)}, u32[]{:S(2)}, u32[]{:S(2)}) collective-permute-start(f32[16,64,256]{2,1,0:T(8,128)S(1)} %multiply_add_fusion.7), channel_id=1, source_target_pairs={{0,16},{16,32},{32,48},{48,64},{64,80},{80,96},{96,112},{112,128},... | collective-permute-start | bytes 3145736 | tf_op jit(solution)/shard_map/while/body/eval_jaxpr/ppermute | solution.py:25
  339.4 23.1 %collective-permute-start = (f32[16,64,256]{2,1,0:T(8,128)S(1)}, f32[16,64,256]{2,1,0:T(8,128)S(1)}, u32[]{:S(2)}, u32[]{:S(2)}) collective-permute-start(f32[16,64,256]{2,1,0:T(8,128)S(1)} %multiply_add_fusion.7), channel_id=1, source_target_pairs={{0,16},{16,32},{32,48},{48,64},{64,80},{80,96},{96,112},{112,128},... | collective-permute-start | bytes 3145736 | tf_op jit(solution)/shard_map/while/body/eval_jaxpr/ppermute | solution.py:25
  362.8 23.1 %collective-permute-start = (f32[16,64,256]{2,1,0:T(8,128)S(1)}, f32[16,64,256]{2,1,0:T(8,128)S(1)}, u32[]{:S(2)}, u32[]{:S(2)}) collective-permute-start(f32[16,64,256]{2,1,0:T(8,128)S(1)} %multiply_add_fusion.7), channel_id=1, source_target_pairs={{0,16},{16,32},{32,48},{48,64},{64,80},{80,96},{96,112},{112,128},... | collective-permute-start | bytes 3145736 | tf_op jit(solution)/shard_map/while/body/eval_jaxpr/ppermute | solution.py:25
  386.1 24.2 %collective-permute-start = (f32[16,64,256]{2,1,0:T(8,128)S(1)}, f32[16,64,256]{2,1,0:T(8,128)S(1)}, u32[]{:S(2)}, u32[]{:S(2)}) collective-permute-start(f32[16,64,256]{2,1,0:T(8,128)S(1)} %multiply_add_fusion.7), channel_id=1, source_target_pairs={{0,16},{16,32},{32,48},{48,64},{64,80},{80,96},{96,112},{112,128},... | collective-permute-start | bytes 3145736 | tf_op jit(solution)/shard_map/while/body/eval_jaxpr/ppermute | solution.py:25
  410.5 25.4 %collective-permute-start = (f32[16,64,256]{2,1,0:T(8,128)S(1)}, f32[16,64,256]{2,1,0:T(8,128)S(1)}, u32[]{:S(2)}, u32[]{:S(2)}) collective-permute-start(f32[16,64,256]{2,1,0:T(8,128)S(1)} %multiply_add_fusion.7), channel_id=1, source_target_pairs={{0,16},{16,32},{32,48},{48,64},{64,80},{80,96},{96,112},{112,128},... | collective-permute-start | bytes 3145736 | tf_op jit(solution)/shard_map/while/body/eval_jaxpr/ppermute | solution.py:25
  436.0 26.5 %collective-permute-start = (f32[16,64,256]{2,1,0:T(8,128)S(1)}, f32[16,64,256]{2,1,0:T(8,128)S(1)}, u32[]{:S(2)}, u32[]{:S(2)}) collective-permute-start(f32[16,64,256]{2,1,0:T(8,128)S(1)} %multiply_add_fusion.7), channel_id=1, source_target_pairs={{0,16},{16,32},{32,48},{48,64},{64,80},{80,96},{96,112},{112,128},... | collective-permute-start | bytes 3145736 | tf_op jit(solution)/shard_map/while/body/eval_jaxpr/ppermute | solution.py:25
  462.7 27.7 %collective-permute-start = (f32[16,64,256]{2,1,0:T(8,128)S(1)}, f32[16,64,256]{2,1,0:T(8,128)S(1)}, u32[]{:S(2)}, u32[]{:S(2)}) collective-permute-start(f32[16,64,256]{2,1,0:T(8,128)S(1)} %multiply_add_fusion.7), channel_id=1, source_target_pairs={{0,16},{16,32},{32,48},{48,64},{64,80},{80,96},{96,112},{112,128},... | collective-permute-start | bytes 3145736 | tf_op jit(solution)/shard_map/while/body/eval_jaxpr/ppermute | solution.py:25
  490.5 27.1 %collective-permute-start = (f32[16,64,256]{2,1,0:T(8,128)S(1)}, f32[16,64,256]{2,1,0:T(8,128)S(1)}, u32[]{:S(2)}, u32[]{:S(2)}) collective-permute-start(f32[16,64,256]{2,1,0:T(8,128)S(1)} %multiply_add_fusion.7), channel_id=1, source_target_pairs={{0,16},{16,32},{32,48},{48,64},{64,80},{80,96},{96,112},{112,128},... | collective-permute-start | bytes 3145736 | tf_op jit(solution)/shard_map/while/body/eval_jaxpr/ppermute | solution.py:25
  517.8 26.2 %collective-permute-start = (f32[16,64,256]{2,1,0:T(8,128)S(1)}, f32[16,64,256]{2,1,0:T(8,128)S(1)}, u32[]{:S(2)}, u32[]{:S(2)}) collective-permute-start(f32[16,64,256]{2,1,0:T(8,128)S(1)} %multiply_add_fusion.7), channel_id=1, source_target_pairs={{0,16},{16,32},{32,48},{48,64},{64,80},{80,96},{96,112},{112,128},... | collective-permute-start | bytes 3145736 | tf_op jit(solution)/shard_map/while/body/eval_jaxpr/ppermute | solution.py:25
  544.1 25.4 %collective-permute-start = (f32[16,64,256]{2,1,0:T(8,128)S(1)}, f32[16,64,256]{2,1,0:T(8,128)S(1)}, u32[]{:S(2)}, u32[]{:S(2)}) collective-permute-start(f32[16,64,256]{2,1,0:T(8,128)S(1)} %multiply_add_fusion.7), channel_id=1, source_target_pairs={{0,16},{16,32},{32,48},{48,64},{64,80},{80,96},{96,112},{112,128},... | collective-permute-start | bytes 3145736 | tf_op jit(solution)/shard_map/while/body/eval_jaxpr/ppermute | solution.py:25
  569.7 24.5 %collective-permute-start = (f32[16,64,256]{2,1,0:T(8,128)S(1)}, f32[16,64,256]{2,1,0:T(8,128)S(1)}, u32[]{:S(2)}, u32[]{:S(2)}) collective-permute-start(f32[16,64,256]{2,1,0:T(8,128)S(1)} %multiply_add_fusion.7), channel_id=1, source_target_pairs={{0,16},{16,32},{32,48},{48,64},{64,80},{80,96},{96,112},{112,128},... | collective-permute-start | bytes 3145736 | tf_op jit(solution)/shard_map/while/body/eval_jaxpr/ppermute | solution.py:25
  594.3 26.5 %collective-permute-start = (f32[16,64,256]{2,1,0:T(8,128)S(1)}, f32[16,64,256]{2,1,0:T(8,128)S(1)}, u32[]{:S(2)}, u32[]{:S(2)}) collective-permute-start(f32[16,64,256]{2,1,0:T(8,128)S(1)} %multiply_add_fusion.7), channel_id=1, source_target_pairs={{0,16},{16,32},{32,48},{48,64},{64,80},{80,96},{96,112},{112,128},... | collective-permute-start | bytes 3145736 | tf_op jit(solution)/shard_map/while/body/eval_jaxpr/ppermute | solution.py:25
  621.0 26.1 %collective-permute-start = (f32[16,64,256]{2,1,0:T(8,128)S(1)}, f32[16,64,256]{2,1,0:T(8,128)S(1)}, u32[]{:S(2)}, u32[]{:S(2)}) collective-permute-start(f32[16,64,256]{2,1,0:T(8,128)S(1)} %multiply_add_fusion.7), channel_id=1, source_target_pairs={{0,16},{16,32},{32,48},{48,64},{64,80},{80,96},{96,112},{112,128},... | collective-permute-start | bytes 3145736 | tf_op jit(solution)/shard_map/while/body/eval_jaxpr/ppermute | solution.py:25
  647.3 18.8 %collective-permute-start = (f32[16,64,256]{2,1,0:T(8,128)S(1)}, f32[16,64,256]{2,1,0:T(8,128)S(1)}, u32[]{:S(2)}, u32[]{:S(2)}) collective-permute-start(f32[16,64,256]{2,1,0:T(8,128)S(1)} %multiply_add_fusion.7), channel_id=1, source_target_pairs={{0,16},{16,32},{32,48},{48,64},{64,80},{80,96},{96,112},{112,128},... | collective-permute-start | bytes 3145736 | tf_op jit(solution)/shard_map/while/body/eval_jaxpr/ppermute | solution.py:25
  667.3 353.0 %all-reduce.6.cloned.1.call-start = ((), (), s32[]{:S(2)}) async-start(), calls=%async_computation.1 | async-start | bytes 2097152 | tf_op jit(solution)/shard_map/psum | solution.py:30
  669.7 168.8 %copy-start.50 = (s32[8]{0:T(128)S(1)}, s32[8]{0:T(128)}, u32[]{:S(2)}) copy-start(s32[8]{0:T(128)} %param.35) | copy-start | bytes 100
  838.3 284.8 %all-gather.2.cloned.1.call-start = ((), (), s32[]{:S(2)}) async-start(), calls=%async_computation.2 | async-start | bytes 8912896 | tf_op jit(solution)/shard_map/all_gather | solution.py:34
  (51 other events, 2625.7 us)
Sparse Core Ops, SparseCore 0:
  667.4 169.6 all-reduce.3
  839.8 180.4 all-reduce.5
  1022.1 100.9 all-gather.1
where the time goes:
time: 1170 us; the launch traced here: 1160 us
  waiting for transfers between devices  663 us (57%)
  blocking collectives  240 us (21%)
  local copies, waits for them, and re-layouts  94.2 us (8%)
  other arithmetic  65.2 us (6%)
  starting transfers between devices  54.3 us (5%)
  matrix products  32.5 us (3%)
  between operations  14.7 us (1%)
    ppermute x18, waiting for transfers between devices, passed_along(): lax.ppermute(value, axis, [(source, source + steps) for source in range(f...  328 us
    psum x2, waiting for transfers between devices, from_root(): return lax.psum(kept, axis)  235 us
    psum x2, blocking collectives, from_root(): return lax.psum(kept, axis)  158 us
    all_gather x1, waiting for transfers between devices, joined(): pieces = jax.tree.map(lambda part: lax.all_gather(part, axis), value)  99.5 us
    all_gather x2, blocking collectives, joined(): pieces = jax.tree.map(lambda part: lax.all_gather(part, axis), value)  81.4 us
    ppermute x18, starting transfers between devices, passed_along(): lax.ppermute(value, axis, [(source, source + steps) for source in range(f...  53.9 us
    dynamic_update_slice x4, local copies, waits for them, and re-layouts, run_spans(): ssm_state, results = lax.scan(span_pass, ssm_state, blocks)  45.9 us
  transfers between devices with their start and end apart: 21, of which 18 were waited for; matrix products, arithmetic and copies ran while one was open for 6% of the time, Pallas kernels for 0%

commit v1 on v0

v1 whole, which is shorter than its diff:
```python
import jax
import jax.numpy as jnp
from jax import lax
from jax.sharding import PartitionSpec as P

HEADS = 256
HDIM = 64
STATE = 256
GROUPS = 8
TAPS = 4
QHEADS = 64
KVHEADS = 8
ADIM = 128
SPAN = 256
STEPS = 2


HIGH = lax.Precision.HIGHEST
NEG = -1e30


def passed_along(value, axis, steps):
    count = lax.axis_size(axis)
    first, last = (max(0, -steps), min(count, count - steps))
    return lax.ppermute(value, axis, [(source, source + steps) for source in range(first, last)])


def causal_conv(leading, source, kernel):
    row_total = source.shape[0]
    padded = jnp.concatenate([leading, source], axis=0)
    accumulated = jnp.zeros_like(source)
    for position in range(TAPS):
        accumulated = accumulated + kernel[position] * padded[position : position + row_total]
    return jax.nn.silu(accumulated)


def decode_conv(leading, fresh, kernel):
    results = []
    for current in range(fresh.shape[0]):
        accumulated = jnp.zeros(fresh.shape[1:], jnp.float32)
        for position in range(TAPS):
            place = current + position
            if place < TAPS - 1:
                term = leading[place][None, :]
            else:
                term = fresh[place - (TAPS - 1)]
            accumulated = accumulated + kernel[position] * term
        results.append(jax.nn.silu(accumulated))
    return jnp.stack(results)


def span_pass(ssm_state, block):
    inputs, entries, readout, log_decay = block
    cumulative = jnp.cumsum(log_decay, axis=1)
    block_size = log_decay.shape[1]
    causal = jnp.arange(block_size)[:, None] >= jnp.arange(block_size)[None, :]
    spreads = cumulative[:, :, None] - cumulative[:, None, :]
    weights = jnp.where(causal[None], jnp.exp(jnp.where(causal[None], spreads, 0.0)), 0.0)
    intersection = jnp.dot(readout, entries.T, precision=HIGH)
    intra_span = jnp.einsum("kts,skp->tkp", weights * intersection[None], inputs, precision=HIGH)
    carried = jnp.exp(cumulative).T[:, :, None] * jnp.einsum(
        "tn,kpn->tkp", readout, ssm_state, precision=HIGH
    )
    remaining = jnp.exp(cumulative[:, -1:] - cumulative)
    updates = jnp.einsum("skp,sn->kpn", inputs * remaining.T[:, :, None], entries, precision=HIGH)
    renewed = jnp.exp(cumulative[:, -1])[:, None, None] * ssm_state + updates
    return (renewed, intra_span + carried)


def decode_mamba(ssm_state, heads_x, heads_b, heads_c, step_dt, rates, gains):
    decays = jnp.exp(-step_dt * rates)
    from_prefix = jnp.einsum("jrhn,hpn->jrhp", heads_c, ssm_state, precision=HIGH)
    results = []
    for current in range(heads_x.shape[0]):
        factor = jnp.ones(decays.shape[1:], jnp.float32)
        accumulated = gains[None, :, None] * heads_x[current]
        for earlier in range(current, -1, -1):
            intersection = jnp.sum(heads_c[current] * heads_b[earlier], axis=-1)
            accumulated = (
                accumulated
                + (factor * step_dt[earlier] * intersection)[..., None] * heads_x[earlier]
            )
            factor = factor * decays[earlier]
        accumulated = accumulated + factor[..., None] * from_prefix[current]
        results.append(accumulated)
    return jnp.stack(results)


def run_spans(inputs, entries, readout, log_decay, ssm_state):
    row_total, heads_here, head_width = inputs.shape
    block_total = row_total // SPAN
    results = []
    for block in range(block_total):
        rows = slice(block * SPAN, (block + 1) * SPAN)
        ssm_state, result = span_pass(
            ssm_state, (inputs[rows], entries[rows], readout[rows], log_decay[:, rows])
        )
        results.append(result)
    return (jnp.concatenate(results, axis=0), ssm_state)


def group_layout(head_begin, head_count):
    per_group = HEADS // GROUPS
    group_count = max(1, head_count // per_group)
    return (head_begin // per_group, group_count, head_count // group_count)


def on_device(
    pre_x,
    pre_b,
    pre_c,
    pre_dt,
    decay_rate,
    skip_gain,
    conv_taps,
    dec_x,
    dec_b,
    dec_c,
    dec_dt,
    dec_query,
    new_kv,
    cache_kv,
    kv_len,
):
    seq_count = lax.axis_size("seq")
    grp_count = lax.axis_size("grp")
    seq_index = lax.axis_index("seq")
    grp_index = lax.axis_index("grp")
    section = pre_x.shape[0]
    local_heads = pre_x.shape[1] // HDIM
    edge = TAPS - 1
    x_offset = HEADS * HDIM
    c_offset = HEADS * HDIM + GROUPS * STATE
    head_begin = grp_index * local_heads
    group_begin, group_count, heads_each = group_layout(head_begin, local_heads)
    source_x = pre_x.astype(jnp.float32)
    group_b = lax.dynamic_slice_in_dim(pre_b, group_begin * STATE, group_count * STATE, 1).astype(
        jnp.float32
    )
    group_c = lax.dynamic_slice_in_dim(pre_c, group_begin * STATE, group_count * STATE, 1).astype(
        jnp.float32
    )
    tail_rows = (source_x[section - edge :], group_b[section - edge :], group_c[section - edge :])
    leading = passed_along(tail_rows, "seq", 1)
    kernel_x = lax.dynamic_slice_in_dim(conv_taps, head_begin * HDIM, local_heads * HDIM, 1)
    kernel_b = lax.dynamic_slice_in_dim(
        conv_taps, x_offset + group_begin * STATE, group_count * STATE, 1
    )
    kernel_c = lax.dynamic_slice_in_dim(
        conv_taps, c_offset + group_begin * STATE, group_count * STATE, 1
    )
    conv_x = causal_conv(leading[0], source_x, kernel_x)
    conv_b = causal_conv(leading[1], group_b, kernel_b)
    conv_c = causal_conv(leading[2], group_c, kernel_c)
    rates = lax.dynamic_slice_in_dim(decay_rate, head_begin, local_heads, 0)
    gains = lax.dynamic_slice_in_dim(skip_gain, head_begin, local_heads, 0)
    log_decay = -pre_dt * rates[:, None]
    head_inputs = conv_x.reshape(section, local_heads, HDIM)
    scaled = head_inputs * pre_dt.T[:, :, None]
    grouped = scaled.reshape(section, group_count, heads_each, HDIM).transpose(1, 0, 2, 3)
    entries = conv_b.reshape(section, group_count, STATE).transpose(1, 0, 2)
    readout = conv_c.reshape(section, group_count, STATE).transpose(1, 0, 2)
    decay_groups = log_decay.reshape(group_count, heads_each, section)
    blank = jnp.zeros((group_count, heads_each, HDIM, STATE), jnp.float32)
    intra_part, closing_local = jax.vmap(run_spans)(grouped, entries, readout, decay_groups, blank)
    local_state = closing_local.reshape(local_heads, HDIM, STATE)
    cumulative = jnp.cumsum(log_decay, axis=1)
    section_decay = cumulative[:, -1]

    rows_here = dec_x.shape[1]
    group_size = QHEADS // KVHEADS
    score_scale = ADIM ** (-0.5)
    positions = cache_kv.shape[2]
    queries = dec_query.reshape(STEPS, rows_here, KVHEADS, group_size, ADIM)
    key_rows = cache_kv[0].reshape(rows_here, positions, KVHEADS, ADIM)
    value_rows = cache_kv[1].reshape(rows_here, positions, KVHEADS, ADIM).astype(jnp.float32)
    scores = (
        jnp.einsum("jrkgd,rckd->jrkgc", queries, key_rows, preferred_element_type=jnp.float32)
        * score_scale
    )
    places = seq_index * positions + jnp.arange(positions)
    usable = (places[None, :] < kv_len[:, None])[None, :, None, None, :]
    scores = jnp.where(usable, scores, NEG)
    peak_local = jnp.max(scores, axis=-1)
    weights = jnp.where(usable, jnp.exp(scores - peak_local[..., None]), 0.0)
    mass_local = jnp.sum(weights, axis=-1)
    summed_local = jnp.einsum("jrkgc,rckd->jrkgd", weights, value_rows, precision=HIGH)
    own_heads = QHEADS // seq_count

    def by_owner(part):
        shaped = part.reshape((STEPS, rows_here, seq_count, own_heads) + part.shape[4:])
        moved = jnp.moveaxis(shaped, 2, 0)
        return moved.reshape(seq_count, -1)

    chunk_heads = local_heads // seq_count
    tail_x_parts = (
        tail_rows[0].reshape(edge, seq_count, chunk_heads * HDIM).transpose(1, 0, 2).reshape(seq_count, -1)
    )
    tail_bc = jnp.concatenate([tail_rows[1], tail_rows[2]], axis=0).reshape(seq_count, -1)
    pieces = [
        local_state.reshape(seq_count, -1),
        section_decay.reshape(seq_count, chunk_heads),
        tail_x_parts,
        tail_bc,
    ]
    sizes = [piece.shape[1] for piece in pieces]
    attn_pieces = [by_owner(peak_local), by_owner(mass_local), by_owner(summed_local)]
    attn_sizes = [piece.shape[1] for piece in attn_pieces]
    payload = jnp.concatenate(pieces + attn_pieces, axis=1)
    width = payload.shape[1]
    padded = -(-width // 128) * 128
    payload = jnp.pad(payload, ((0, 0), (0, padded - width)))
    arrived = lax.all_to_all(payload, "seq", 0, 0, tiled=True)
    bounds = [0]
    for size in sizes + attn_sizes:
        bounds.append(bounds[-1] + size)
    got = [arrived[:, bounds[i] : bounds[i + 1]] for i in range(len(bounds) - 1)]
    states_in, decays_in, tail_x_in, tail_bc_in, peak_in, mass_in, summed_in = got

    carry = jnp.zeros((chunk_heads, HDIM * STATE), jnp.float32)
    entering = []
    states_in = states_in.reshape(seq_count, chunk_heads, HDIM * STATE)
    for source in range(seq_count):
        entering.append(carry)
        carry = jnp.exp(decays_in[source])[:, None] * carry + states_in[source]
    entering = jnp.stack(entering).reshape(seq_count, -1)
    returned = lax.all_to_all(entering, "seq", 0, 0, tiled=True)
    incoming = returned.reshape(local_heads, HDIM, STATE)

    handoff = jnp.concatenate(
        [carry.reshape(-1), tail_x_in[seq_count - 1], tail_bc_in[seq_count - 1]], axis=0
    )
    swap = [
        (a * grp_count + b, b * grp_count + a) for a in range(seq_count) for b in range(grp_count)
    ]
    swapped = lax.ppermute(handoff, ("seq", "grp"), swap)
    gathered = lax.all_gather(swapped, "grp")
    state_size = chunk_heads * HDIM * STATE
    tail_size = tail_x_in.shape[1]
    state_heads = HEADS // seq_count
    prefix_state = gathered[:, :state_size].reshape(state_heads, HDIM, STATE)
    prefix_tail = (
        gathered[:, state_size : state_size + tail_size]
        .reshape(grp_count, edge, chunk_heads * HDIM)
        .transpose(1, 0, 2)
        .reshape(edge, state_heads * HDIM)
    )
    dgroup_width = tail_rows[1].shape[1]
    tail_bc_all = gathered[:, state_size + tail_size :].reshape(2 * edge, dgroup_width)
    tail_b = tail_bc_all[:edge]
    tail_c = tail_bc_all[edge:]

    incoming_groups = incoming.reshape(group_count, heads_each, HDIM, STATE)
    from_before = jnp.einsum("gsn,gkpn->gskp", readout, incoming_groups, precision=HIGH)
    decay_factor = jnp.exp(cumulative).reshape(group_count, heads_each, section).transpose(0, 2, 1)
    combined = intra_part + decay_factor[..., None] * from_before
    combined = (
        combined.transpose(1, 0, 2, 3).reshape(section, local_heads, HDIM)
        + gains[None, :, None] * head_inputs
    )
    pre_y = combined.reshape(section, local_heads * HDIM).astype(jnp.bfloat16)

    dec_begin = seq_index * state_heads
    dgroup_begin, dgroup_count, dheads_each = group_layout(dec_begin, state_heads)
    kernel_dx = lax.dynamic_slice_in_dim(conv_taps, dec_begin * HDIM, state_heads * HDIM, 1)
    kernel_db = lax.dynamic_slice_in_dim(
        conv_taps, x_offset + dgroup_begin * STATE, dgroup_count * STATE, 1
    )
    kernel_dc = lax.dynamic_slice_in_dim(
        conv_taps, c_offset + dgroup_begin * STATE, dgroup_count * STATE, 1
    )
    step_x = decode_conv(prefix_tail, dec_x.astype(jnp.float32), kernel_dx)
    step_b = decode_conv(
        tail_b,
        lax.dynamic_slice_in_dim(dec_b, dgroup_begin * STATE, dgroup_count * STATE, 2).astype(
            jnp.float32
        ),
        kernel_db,
    )
    step_c = decode_conv(
        tail_c,
        lax.dynamic_slice_in_dim(dec_c, dgroup_begin * STATE, dgroup_count * STATE, 2).astype(
            jnp.float32
        ),
        kernel_dc,
    )
    heads_x = step_x.reshape(STEPS, rows_here, state_heads, HDIM)
    heads_b = jnp.repeat(step_b.reshape(STEPS, rows_here, dgroup_count, STATE), dheads_each, axis=2)
    heads_c = jnp.repeat(step_c.reshape(STEPS, rows_here, dgroup_count, STATE), dheads_each, axis=2)
    dec_rates = lax.dynamic_slice_in_dim(decay_rate, dec_begin, state_heads, 0)
    dec_gains = lax.dynamic_slice_in_dim(skip_gain, dec_begin, state_heads, 0)
    mamba_out = decode_mamba(prefix_state, heads_x, heads_b, heads_c, dec_dt, dec_rates, dec_gains)
    dec_y = mamba_out.reshape(STEPS, rows_here, state_heads * HDIM).astype(jnp.bfloat16)

    peak_in = peak_in.reshape(seq_count, STEPS, rows_here, own_heads)
    mass_in = mass_in.reshape(seq_count, STEPS, rows_here, own_heads)
    summed_in = summed_in.reshape(seq_count, STEPS, rows_here, own_heads, ADIM)
    peak_cache = jnp.max(peak_in, axis=0)
    part_scale = jnp.exp(peak_in - peak_cache[None])
    mass_cache = jnp.sum(mass_in * part_scale, axis=0)
    summed_cache = jnp.sum(summed_in * part_scale[..., None], axis=0)
    head_start = seq_index * own_heads
    new_keys = new_kv[0].reshape(STEPS, rows_here, KVHEADS, ADIM)
    new_values = new_kv[1].reshape(STEPS, rows_here, KVHEADS, ADIM).astype(jnp.float32)
    new_scores = (
        jnp.einsum("jrkgd,irkd->jrkgi", queries, new_keys, preferred_element_type=jnp.float32)
        * score_scale
    )
    allowed = (jnp.arange(STEPS)[None, :] <= jnp.arange(STEPS)[:, None])[:, None, None, None, :]
    new_scores = jnp.where(allowed, new_scores, NEG)
    new_scores = lax.dynamic_slice_in_dim(
        new_scores.reshape(STEPS, rows_here, QHEADS, STEPS), head_start, own_heads, 2
    )
    allowed_heads = (jnp.arange(STEPS)[None, :] <= jnp.arange(STEPS)[:, None])[:, None, None, :]
    head_kv = (head_start + jnp.arange(own_heads)) // group_size
    pick = (head_kv[:, None] == jnp.arange(KVHEADS)[None, :]).astype(jnp.float32)
    own_values = jnp.einsum("hk,irkd->irhd", pick, new_values, precision=HIGH)
    peak_total = jnp.maximum(peak_cache, jnp.max(new_scores, axis=-1))
    cache_scale = jnp.exp(peak_cache - peak_total)
    new_weights = jnp.where(allowed_heads, jnp.exp(new_scores - peak_total[..., None]), 0.0)
    mass_total = mass_cache * cache_scale + jnp.sum(new_weights, axis=-1)
    summed_total = summed_cache * cache_scale[..., None] + jnp.einsum(
        "jrhi,irhd->jrhd", new_weights, own_values, precision=HIGH
    )
    attn_out = (
        (summed_total / mass_total[..., None])
        .reshape(STEPS, rows_here, own_heads * ADIM)
        .astype(jnp.bfloat16)
    )
    return (pre_y, dec_y, attn_out)


def solution(mesh):
    in_specs = (
        P("seq", "grp"),
        P("seq", None),
        P("seq", None),
        P("grp", "seq"),
        P(),
        P(),
        P(),
        P(None, "grp", "seq"),
        P(None, "grp", None),
        P(None, "grp", None),
        P(None, "grp", "seq"),
        P(None, "grp", None),
        P(None, None, "grp", None),
        P(None, "grp", "seq", None),
        P("grp"),
    )
    out_specs = (P("seq", "grp"), P(None, "grp", "seq"), P(None, "grp", "seq"))
    return jax.shard_map(
        on_device, mesh=mesh, in_specs=in_specs, out_specs=out_specs, check_vma=False
    )
```

time: 1170 us -> 589 us (0.50)
  waiting for transfers between devices: 663 us -> 196 us
  blocking collectives: 240 us -> 0 us
  other arithmetic: 65.2 us -> 201 us
  local copies, waits for them, and re-layouts: 94.2 us -> 77.1 us
    ppermute x18 -> x3, waiting for transfers between devices: 328 us -> 0.01 us  [passed_along(): lax.ppermute(value, axis, [(source, source + steps) for source in range(f...]
    psum x2 -> x0, waiting for transfers between devices: 235 us -> none  [from_root(): return lax.psum(kept, axis)]
    unnamed x3 -> x2, waiting for transfers between devices: 0.05 us -> 174 us
    psum x2 -> x0, blocking collectives: 158 us -> none  [from_root(): return lax.psum(kept, axis)]
    add x45 -> x3, other arithmetic: 25.9 us -> 151 us  [on_device(): carry = jnp.exp(decays_in[source])[:, None] * carry + states_in[source]]
    all_gather x1 -> x0, waiting for transfers between devices: 99.5 us -> none  [joined(): pieces = jax.tree.map(lambda part: lax.all_gather(part, axis), value)]
    all_gather x2 -> x0, blocking collectives: 81.4 us -> none  [joined(): pieces = jax.tree.map(lambda part: lax.all_gather(part, axis), value)]
    dynamic_update_slice x4 -> x0, local copies, waits for them, and re-layouts: 45.9 us -> none  [run_spans(): ssm_state, results = lax.scan(span_pass, ssm_state, blocks)]
  transfers between devices with their start and end apart: 21 -> 7, of which waited for: 18 -> 2; matrix products, arithmetic and copies ran while one was open for 6% -> 50% of each run, Pallas kernels for 0% -> 0%
where the time goes in v1:
time: 589 us; the launch traced here: 578 us
  other arithmetic  201 us (34%)
  waiting for transfers between devices  196 us (33%)
  local copies, waits for them, and re-layouts  77.1 us (13%)
  starting transfers between devices  44.8 us (8%)
  matrix products  33.5 us (6%)
  between operations  26.4 us (4%)
    unnamed x2, waiting for transfers between devices  174 us
    add x3, other arithmetic, on_device(): carry = jnp.exp(decays_in[source])[:, None] * carry + states_in[source]  151 us
    all_to_all x1, waiting for transfers between devices, on_device(): arrived = lax.all_to_all(payload, 'seq', 0, 0, tiled=True)  21.3 us
    unnamed x98, local copies, waits for them, and re-layouts  20.7 us
    dot_general x2, matrix products, span_pass(): jnp.einsum('kts,skp->tkp', weights * intersection[None], inputs, precisio...  13.9 us
    all_to_all x1, starting transfers between devices, on_device(): returned = lax.all_to_all(entering, 'seq', 0, 0, tiled=True)  13.7 us
    ppermute x1, starting transfers between devices, on_device(): swapped = lax.ppermute(handoff, ('seq', 'grp'), swap)  13.1 us
  transfers between devices with their start and end apart: 7, of which 2 were waited for; matrix products, arithmetic and copies ran while one was open for 50% of the time, Pallas kernels for 0%

profile of v1, /device:TPU:8, one launch (start us, length us, event | category | flops | bytes accessed | tf_op | source)
XLA Modules:
  0.0 578.0 jit_solution(7144240537419114576)
XLA Ops:
  8.8 3.5 collective-permute-start.2
  13.0 3.2 collective-permute-start
  18.6 3.5 collective-permute-start.1
  26.9 2.8 convert_element_type.33
  49.5 5.1 divide_multiply_fusion
  64.1 2.4 concatenate.35
  68.1 2.3 all_to_all.12
  70.4 7.8 %all-to-all-start = ((f32[16,1,25088]{2,1,0:T(1,128)}), f32[16,1,25088]{2,1,0:T(1,128)}, u32[]{:S(2)}, u32[]{:S(2)}) async-start(f32[16,1,25088]{2,1,0:T(1,128)} %all_to_all.12), calls=%async_computation | async-start | bytes 3211264 | tf_op jit(solution)/shard_map/all_to_all | solution.py:213
  88.7 21.3 %all-to-all-done = f32[16,1,25088]{2,1,0:T(1,128)} async-done(((f32[16,1,25088]{2,1,0:T(1,128)}), f32[16,1,25088]{2,1,0:T(1,128)}, u32[]{:S(2)}, u32[]{:S(2)}) %all-to-all-start) | async-done | bytes 1605664 | tf_op jit(solution)/shard_map/all_to_all | solution.py:213
  110.1 9.3 %copy.199 = f32[16,1,25088]{0,2,1:T(8,128)} copy(f32[16,1,25088]{2,1,0:T(1,128)} %all-to-all-done) | data formatting | bytes 3211264 | tf_op jit(solution)/shard_map/all_to_all | solution.py:213
  137.2 73.9 %slice_add_fusion.2 = (f32[1,16384]{0,1:T(8,128)}, f32[1,16384]{0,1:T(8,128)}, f32[1,16384]{0,1:T(8,128)}, f32[1,16384]{0,1:T(8,128)}, f32[1,16384]{0,1:T(8,128)}, /*index=5*/f32[1,16384]{0,1:T(8,128)}, f32[1,16384]{0,1:T(8,128)}) fusion(f32[16,25088]{0,1:T(8,128)} %bitcast.323, f32[]{:T(128)} %bitcast.78, f32[]{:T(128)} %bitcast.77, f32[]{:T(128)} %bitcast.75, ...), kind=kLoop, calls=%fused_computation.3 | loop fusion | flops 442368 | bytes 1376312 | tf_op jit(solution)/shard_map/add | solution.py:225
  211.1 53.3 %fusion = (f32[16384]{0:T(1024)}, f32[16384]{0:T(1024)S(1)}, f32[16384]{0:T(1024)S(1)}, f32[16384]{0:T(1024)S(1)}, f32[16384]{0:T(1024)}, /*index=5*/f32[16384]{...) fusion(f32[16,25088]{0,1:T(8,128)} %bitcast.324, ...), kind=kLoop, calls=%fused_computation.1 | loop fusion | flops 196608 | bytes 1441816 | tf_op jit(solution)/shard_map/add | solution.py:225
  265.9 13.1 %collective-permute-start.3 = (f32[16672]{0:T(1024)}, f32[16672]{0:T(1024)}, u32[]{:S(2)}, u32[]{:S(2)}) collective-permute-start(f32[16672]{0:T(1024)} %concatenate.36), channel_id=1, source_target_pairs={{0,0},{1,16},{2,32},{3,48},{4,64},{5,80},{6,96},{7,112},{8,128},{9... | collective-permute-start | bytes 200072 | tf_op jit(solution)/shard_map/ppermute | solution.py:236
  279.1 23.7 %fusion.16 = (f32[16384]{0:T(1024)S(1)}, f32[16384]{0:T(1024)S(1)}, f32[16384]{0:T(1024)S(1)}, f32[16384]{0:T(1024)S(1)}, f32[16384]{0:T(1024)S(1)}) fusion(f32[16,25088]{0,1:T(8,128)} %bitcast.325, f32[1,16384]{0,1:T(8,128)} %get-tuple-element.44, f32[]{:T(128)} %bitcast.69, f32[1,16384]{0,1:T(8,128)} %get-tuple-element.45, f32[]{:T(128)} %bitcast.67, ...), kind=kLoop, calls=%fused_computation.35 | loop fusion | flops 81920 | bytes 655372 | tf_op jit(solution)/shard_map/add | solution.py:225
  319.3 3.3 fusion.2
  322.8 13.7 %all-to-all-start.1 = ((f32[16,1,16384]{2,1,0:T(1,128)}), f32[16,1,16384]{2,1,0:T(1,128)}, u32[]{:S(2)}, u32[]{:S(2)}) async-start(f32[16,1,16384]{2,1,0:T(1,128)} %constant_dynamic-update-slice_fusion), calls=%async_computation.1 | async-start | bytes 2097152 | tf_op jit(solution)/shard_map/all_to_all | solution.py:227
  338.4 174.4 %all-reduce.4.cloned.1.call-done = f32[266752]{0:T(1024)} async-done(((f32[266752]{0:T(1024)}), f32[266752]{0:T(1024)}) %all-reduce.4.cloned.1.call-update) | async-done | bytes 1067024
  512.8 2.9 reshape.1119
  539.8 7.1 %fusion.57 = f32[256,16,64]{0,2,1:T(8,128)} fusion(f32[1,256,16,64]{1,3,2,0:T(8,128)S(1)} %fusion.47, f32[256,256]{1,0:T(8,128)S(1)} %fusion.105, f32[16,256]{1,0:T(8,128)} %bitcast_add_fusion.2, pred[256,256]{1,0:T(8,128)(4,1)S(1)} %copy-done.19, f32[1,512,16,64]{1,3,2,0:T(8,128)} %copy-done.2), kind=kOutput, calls=%fused_computation.74 | convolution fusion | flops 809762816 | bytes 3506176 | tf_op jit(solution)/shard_map/vmap(kts,skp->tkp)/dot_general | solution.py:60
  546.9 6.8 %fusion.51 = f32[256,16,64]{0,2,1:T(8,128)} fusion(f32[1,256,16,64]{1,3,2,0:T(8,128)S(1)} %fusion.46, f32[256,256]{1,0:T(8,128)S(1)} %fusion.101, f32[16,256]{1,0:T(8,128)} %bitcast_add_fusion.1, pred[256,256]{1,0:T(8,128)(4,1)S(1)} %copy-done.19, f32[1,512,16,64]{1,3,2,0:T(8,128)S(1)} %copy-done.3), kind=kOutput, calls=%fused_computation.72 | convolution fusion | flops 809762816 | bytes 3506176 | tf_op jit(solution)/shard_map/vmap(kts,skp->tkp)/dot_general | solution.py:60
  553.7 4.7 reduce.29
  560.0 4.8 maximum_add_fusion
  564.8 2.9 copy.200
  567.7 3.1 add_convert_fusion
  (250 shorter events, 102.7 us)
Async XLA Ops:
  7.2 33.0 %copy-start = (bf16[2,8,8192]{2,1,0:T(8,128)(2,1)S(1)}, bf16[2,8,8192]{2,1,0:T(8,128)(2,1)}, u32[]{:S(2)}) copy-start(bf16[2,8,8192]{2,1,0:T(8,128)(2,1)} %param.26) | copy-start | bytes 786436
  8.8 38.7 %collective-permute-start.2 = (f32[3,256]{1,0:T(4,128)}, f32[3,256]{1,0:T(4,128)}, u32[]{:S(2)}, u32[]{:S(2)}) collective-permute-start(f32[3,256]{1,0:T(4,128)} %slice.609), channel_id=1, source_target_pairs={{0,16},{16,32},{32,48},{48,64},{64,80},{80,96},{96,112},{112,128},... | collective-permute-start | bytes 9224 | tf_op jit(solution)/shard_map/ppermute | solution.py:25
  13.0 36.5 %collective-permute-start = (f32[3,1024]{1,0:T(4,128)S(1)}, f32[3,1024]{1,0:T(4,128)}, u32[]{:S(2)}, u32[]{:S(2)}) collective-permute-start(f32[3,1024]{1,0:T(4,128)S(1)} %slice.595), channel_id=1, source_target_pairs={{0,16},{16,32},{32,48},{48,64},{64,80},{80,96},{96,112},{112,128},... | collective-permute-start | bytes 36872 | tf_op jit(solution)/shard_map/ppermute | solution.py:25
  18.6 514.2 %collective-permute-start.1 = (f32[3,256]{1,0:T(4,128)}, f32[3,256]{1,0:T(4,128)}, u32[]{:S(2)}, u32[]{:S(2)}) collective-permute-start(f32[3,256]{1,0:T(4,128)} %slice.603), channel_id=1, source_target_pairs={{0,16},{16,32},{32,48},{48,64},{64,80},{80,96},{96,112},{112,128},... | collective-permute-start | bytes 9224 | tf_op jit(solution)/shard_map/ppermute | solution.py:25
  62.5 18.9 %copy-start.28 = (f32[16]{0:T(128)S(1)}, f32[16]{0:T(128)}, u32[]{:S(2)}) copy-start(f32[16]{0:T(128)} %get-tuple-element.108) | copy-start | bytes 196
  62.5 19.6 %copy-start.33 = (u32[256]{0:T(256)S(1)}, u32[256]{0:T(256)}, u32[]{:S(2)}) copy-start(u32[256]{0:T(256)} %constant.118) | copy-start | bytes 3076
  62.5 24.7 %copy-start.16 = (bf16[2,8,8,128]{3,1,2,0:T(8,128)(2,1)S(1)}, bf16[2,8,8,128]{3,1,2,0:T(8,128)(2,1)}, u32[]{:S(2)}) copy-start(bf16[2,8,8,128]{3,1,2,0:T(8,128)(2,1)} %get-tuple-element.93) | copy-start | bytes 98308
  70.4 39.7 %all-to-all-start = ((f32[16,1,25088]{2,1,0:T(1,128)}), f32[16,1,25088]{2,1,0:T(1,128)}, u32[]{:S(2)}, u32[]{:S(2)}) async-start(f32[16,1,25088]{2,1,0:T(1,128)} %all_to_all.12), calls=%async_computation | async-start | bytes 3211264 | tf_op jit(solution)/shard_map/all_to_all | solution.py:213
  78.1 434.6 %all-reduce.4.cloned.1.call-start = ((), (), s32[]{:S(2)}) async-start(), calls=%async_computation.2 | async-start | bytes 2138112
  120.8 90.2 %copy-start.26 = (f32[64]{0:T(128)}, f32[64]{0:T(128)S(1)}, u32[]{:S(2)}) copy-start(f32[64]{0:T(128)S(1)} %get-tuple-element.51) | copy-start | bytes 772
  265.9 48.2 %collective-permute-start.3 = (f32[16672]{0:T(1024)}, f32[16672]{0:T(1024)}, u32[]{:S(2)}, u32[]{:S(2)}) collective-permute-start(f32[16672]{0:T(1024)} %concatenate.36), channel_id=1, source_target_pairs={{0,0},{1,16},{2,32},{3,48},{4,64},{5,80},{6,96},{7,112},{8,128},{9... | collective-permute-start | bytes 200072 | tf_op jit(solution)/shard_map/ppermute | solution.py:236
  279.1 26.9 %copy-start.10 = (f32[16384]{0:T(1024)S(1)}, f32[16384]{0:T(1024)}, u32[]{:S(2)}) copy-start(f32[16384]{0:T(1024)} %get-tuple-element.13) | copy-start | bytes 196612
  279.1 27.5 %copy-start.9 = (f32[16384]{0:T(1024)S(1)}, f32[16384]{0:T(1024)}, u32[]{:S(2)}) copy-start(f32[16384]{0:T(1024)} %get-tuple-element.8) | copy-start | bytes 196612
  279.1 28.2 %copy-start.8 = (f32[16384]{0:T(1024)S(1)}, f32[16384]{0:T(1024)}, u32[]{:S(2)}) copy-start(f32[16384]{0:T(1024)} %get-tuple-element.14) | copy-start | bytes 196612
  279.1 28.8 %copy-start.7 = (f32[16384]{0:T(1024)S(1)}, f32[16384]{0:T(1024)}, u32[]{:S(2)}) copy-start(f32[16384]{0:T(1024)} %get-tuple-element.7) | copy-start | bytes 196612
  279.1 33.1 %copy-start.27 = (f32[64]{0:T(128)S(1)}, f32[64]{0:T(128)}, u32[]{:S(2)}) copy-start(f32[64]{0:T(128)} %copy-done.26) | copy-start | bytes 772
  314.1 216.9 %copy-start.11 = (f32[1,8,16,64]{3,2,1,0:T(8,128)S(1)}, f32[1,8,16,64]{3,2,1,0:T(8,128)}, u32[]{:S(2)}) copy-start(f32[1,8,16,64]{3,2,1,0:T(8,128)} %squeeze.22) | copy-start | bytes 98308
  314.1 216.9 %copy-start.12 = (f32[1,8,16,64]{3,2,1,0:T(8,128)S(1)}, f32[1,8,16,64]{3,2,1,0:T(8,128)}, u32[]{:S(2)}) copy-start(f32[1,8,16,64]{3,2,1,0:T(8,128)} %squeeze.24) | copy-start | bytes 98308
  316.9 218.1 %copy-start.22 = (f32[1,256,16]{1,2,0:T(8,128)S(1)}, f32[1,256,16]{1,2,0:T(8,128)}, u32[]{:S(2)}) copy-start(f32[1,256,16]{1,2,0:T(8,128)} %copy.311) | copy-start | bytes 49156
  319.3 216.7 %copy-start.17 = (f32[1,256,16]{1,2,0:T(8,128)S(1)}, f32[1,256,16]{1,2,0:T(8,128)}, u32[]{:S(2)}) copy-start(f32[1,256,16]{1,2,0:T(8,128)} %copy.310) | copy-start | bytes 49156
  322.8 216.9 %copy-start.19 = (pred[256,256]{1,0:T(8,128)(4,1)S(1)}, pred[256,256]{1,0:T(8,128)(4,1)}, u32[]{:S(2)}) copy-start(pred[256,256]{1,0:T(8,128)(4,1)} %iota_compare_fusion) | copy-start | bytes 196612
  322.8 230.8 %all-to-all-start.1 = ((f32[16,1,16384]{2,1,0:T(1,128)}), f32[16,1,16384]{2,1,0:T(1,128)}, u32[]{:S(2)}, u32[]{:S(2)}) async-start(f32[16,1,16384]{2,1,0:T(1,128)} %constant_dynamic-update-slice_fusion), calls=%async_computation.1 | async-start | bytes 2097152 | tf_op jit(solution)/shard_map/all_to_all | solution.py:227
  539.8 20.2 %copy-start.5 = (f32[512,256]{1,0:T(8,128)S(1)}, f32[512,256]{1,0:T(8,128)}, u32[]{:S(2)}) copy-start(f32[512,256]{1,0:T(8,128)} %copy-done.4) | copy-start | bytes 1572868
  539.8 20.2 %copy-start.14 = (f32[1,16,512]{2,1,0:T(8,128)S(1)}, f32[1,16,512]{2,1,0:T(8,128)}, u32[]{:S(2)}) copy-start(f32[1,16,512]{2,1,0:T(8,128)} %exp.245) | copy-start | bytes 98308
  (17 other events, 189.3 us)
Sparse Core Ops, SparseCore 0:
  317.0 195.7 all-reduce.3

commit v2 on v1

--- a/solution.py
+++ b/solution.py
@@ -17,6 +17,29 @@
 
 HIGH = lax.Precision.HIGHEST
 NEG = -1e30
+
+
+LANES = 128
+
+
+def exchanged(pieces, axis):
+    count = pieces[0].shape[0]
+    sizes = [piece.shape[1] for piece in pieces]
+    rows = [-(-size // LANES) for size in sizes]
+    packed = jnp.concatenate(
+        [
+            jnp.pad(piece, ((0, 0), (0, row * LANES - size))).reshape(count, row, LANES)
+            for piece, size, row in zip(pieces, sizes, rows)
+        ],
+        axis=1,
+    )
+    arrived = lax.all_to_all(packed, axis, 0, 0, tiled=False)
+    results = []
+    begin = 0
+    for size, row in zip(sizes, rows):
+        results.append(arrived[:, begin : begin + row].reshape(count, row * LANES)[:, :size])
+        begin += row
+    return results
 
 
 def passed_along(value, axis, steps):
@@ -87,7 +110,7 @@
 
 
 def run_spans(inputs, entries, readout, log_decay, ssm_state):
-    row_total, heads_here, head_width = inputs.shape
+    row_total, _, _ = inputs.shape
     block_total = row_total // SPAN
     results = []
     for block in range(block_total):
@@ -203,40 +226,37 @@
         tail_x_parts,
         tail_bc,
     ]
-    sizes = [piece.shape[1] for piece in pieces]
-    attn_pieces = [by_owner(peak_local), by_owner(mass_local), by_owner(summed_local)]
-    attn_sizes = [piece.shape[1] for piece in attn_pieces]
-    payload = jnp.concatenate(pieces + attn_pieces, axis=1)
-    width = payload.shape[1]
-    padded = -(-width // 128) * 128
-    payload = jnp.pad(payload, ((0, 0), (0, padded - width)))
-    arrived = lax.all_to_all(payload, "seq", 0, 0, tiled=True)
-    bounds = [0]
-    for size in sizes + attn_sizes:
-        bounds.append(bounds[-1] + size)
-    got = [arrived[:, bounds[i] : bounds[i + 1]] for i in range(len(bounds) - 1)]
-    states_in, decays_in, tail_x_in, tail_bc_in, peak_in, mass_in, summed_in = got
-
-    carry = jnp.zeros((chunk_heads, HDIM * STATE), jnp.float32)
-    entering = []
-    states_in = states_in.reshape(seq_count, chunk_heads, HDIM * STATE)
-    for source in range(seq_count):
-        entering.append(carry)
-        carry = jnp.exp(decays_in[source])[:, None] * carry + states_in[source]
-    entering = jnp.stack(entering).reshape(seq_count, -1)
-    returned = lax.all_to_all(entering, "seq", 0, 0, tiled=True)
+    peak_in, mass_in, summed_in = exchanged(
+        [by_owner(peak_local), by_owner(mass_local), by_owner(summed_local)], "seq"
+    )
+    states_in, decays_in, tail_x_in, tail_bc_in = exchanged(pieces, "seq")
+
+    states_in = states_in.reshape(seq_count, chunk_heads, LANES, -1)
+    decays_in = decays_in[:, :chunk_heads]
+    after = jnp.arange(seq_count + 1)[:, None, None]
+    source = jnp.arange(seq_count)[None, :, None]
+    between = jnp.arange(seq_count)[None, None, :]
+    spans = ((source < between) & (between < after)).astype(jnp.float32)
+    exponents = jnp.sum(spans[None] * decays_in.T[:, None, None, :], axis=-1)
+    carry_weights = jnp.where((source < after)[None, :, :, 0], jnp.exp(exponents), 0.0)
+    carried_all = jnp.einsum("has,shrc->ahrc", carry_weights, states_in, precision=HIGH)
+    entering = carried_all[:seq_count].reshape(seq_count, -1, LANES)
+    carry = carried_all[seq_count]
+    returned = lax.all_to_all(entering, "seq", 0, 0, tiled=False)
     incoming = returned.reshape(local_heads, HDIM, STATE)
 
+    state_size = chunk_heads * HDIM * STATE
+    tail_size = tail_x_parts.shape[1]
     handoff = jnp.concatenate(
         [carry.reshape(-1), tail_x_in[seq_count - 1], tail_bc_in[seq_count - 1]], axis=0
     )
+    handoff = jnp.pad(handoff, (0, -handoff.shape[0] % LANES)).reshape(-1, LANES)
     swap = [
         (a * grp_count + b, b * grp_count + a) for a in range(seq_count) for b in range(grp_count)
     ]
     swapped = lax.ppermute(handoff, ("seq", "grp"), swap)
-    gathered = lax.all_gather(swapped, "grp")
-    state_size = chunk_heads * HDIM * STATE
-    tail_size = tail_x_in.shape[1]
+    copies = jnp.broadcast_to(swapped[None], (grp_count,) + swapped.shape)
+    gathered = lax.all_to_all(copies, "grp", 0, 0, tiled=False).reshape(grp_count, -1)
     state_heads = HEADS // seq_count
     prefix_state = gathered[:, :state_size].reshape(state_heads, HDIM, STATE)
     prefix_tail = (
@@ -246,7 +266,10 @@
         .reshape(edge, state_heads * HDIM)
     )
     dgroup_width = tail_rows[1].shape[1]
-    tail_bc_all = gathered[:, state_size + tail_size :].reshape(2 * edge, dgroup_width)
+    bc_size = 2 * edge * dgroup_width // grp_count
+    tail_bc_all = gathered[:, state_size + tail_size : state_size + tail_size + bc_size].reshape(
+        2 * edge, dgroup_width
+    )
     tail_b = tail_bc_all[:edge]
     tail_c = tail_bc_all[edge:]
 
@@ -292,6 +315,22 @@
     mamba_out = decode_mamba(prefix_state, heads_x, heads_b, heads_c, dec_dt, dec_rates, dec_gains)
     dec_y = mamba_out.reshape(STEPS, rows_here, state_heads * HDIM).astype(jnp.bfloat16)
 
+    head_start = seq_index * own_heads
+    new_keys = new_kv[0].reshape(STEPS, rows_here, KVHEADS, ADIM)
+    new_values = new_kv[1].reshape(STEPS, rows_here, KVHEADS, ADIM).astype(jnp.float32)
+    new_scores = (
+        jnp.einsum("jrkgd,irkd->jrkgi", queries, new_keys, preferred_element_type=jnp.float32)
+        * score_scale
+    )
+    allowed = (jnp.arange(STEPS)[None, :] <= jnp.arange(STEPS)[:, None])[:, None, None, None, :]
+    new_scores = jnp.where(allowed, new_scores, NEG)
+    new_scores = lax.dynamic_slice_in_dim(
+        new_scores.reshape(STEPS, rows_here, QHEADS, STEPS), head_start, own_heads, 2
+    )
+    allowed_heads = (jnp.arange(STEPS)[None, :] <= jnp.arange(STEPS)[:, None])[:, None, None, :]
+    head_kv = (head_start + jnp.arange(own_heads)) // group_size
+    pick = (head_kv[:, None] == jnp.arange(KVHEADS)[None, :]).astype(jnp.float32)
+    own_values = jnp.einsum("hk,irkd->irhd", pick, new_values, precision=HIGH)
     peak_in = peak_in.reshape(seq_count, STEPS, rows_here, own_heads)
     mass_in = mass_in.reshape(seq_count, STEPS, rows_here, own_heads)
     summed_in = summed_in.reshape(seq_count, STEPS, rows_here, own_heads, ADIM)
@@ -299,22 +338,6 @@
     part_scale = jnp.exp(peak_in - peak_cache[None])
     mass_cache = jnp.sum(mass_in * part_scale, axis=0)
     summed_cache = jnp.sum(summed_in * part_scale[..., None], axis=0)
-    head_start = seq_index * own_heads
-    new_keys = new_kv[0].reshape(STEPS, rows_here, KVHEADS, ADIM)
-    new_values = new_kv[1].reshape(STEPS, rows_here, KVHEADS, ADIM).astype(jnp.float32)
-    new_scores = (
-        jnp.einsum("jrkgd,irkd->jrkgi", queries, new_keys, preferred_element_type=jnp.float32)
-        * score_scale
-    )
-    allowed = (jnp.arange(STEPS)[None, :] <= jnp.arange(STEPS)[:, None])[:, None, None, None, :]
-    new_scores = jnp.where(allowed, new_scores, NEG)
-    new_scores = lax.dynamic_slice_in_dim(
-        new_scores.reshape(STEPS, rows_here, QHEADS, STEPS), head_start, own_heads, 2
-    )
-    allowed_heads = (jnp.arange(STEPS)[None, :] <= jnp.arange(STEPS)[:, None])[:, None, None, :]
-    head_kv = (head_start + jnp.arange(own_heads)) // group_size
-    pick = (head_kv[:, None] == jnp.arange(KVHEADS)[None, :]).astype(jnp.float32)
-    own_values = jnp.einsum("hk,irkd->irhd", pick, new_values, precision=HIGH)
     peak_total = jnp.maximum(peak_cache, jnp.max(new_scores, axis=-1))
     cache_scale = jnp.exp(peak_cache - peak_total)
     new_weights = jnp.where(allowed_heads, jnp.exp(new_scores - peak_total[..., None]), 0.0)
@@ -349,6 +372,5 @@
         P("grp"),
     )
     out_specs = (P("seq", "grp"), P(None, "grp", "seq"), P(None, "grp", "seq"))
-    return jax.shard_map(
-        on_device, mesh=mesh, in_specs=in_specs, out_specs=out_specs, check_vma=False
-    )
+
+    return jax.shard_map(on_device, mesh=mesh, in_specs=in_specs, out_specs=out_specs, check_vma=False)

time: 589 us -> 225 us (0.38); the launches traced: 578 us -> 221 us
  other arithmetic: 201 us -> 38.2 us
  waiting for transfers between devices: 196 us -> 37.1 us
  between operations: 26.4 us -> 1.65 us
  local copies, waits for them, and re-layouts: 77.1 us -> 58.5 us
  starting transfers between devices: 44.8 us -> 52.5 us
    unnamed x2 -> x0, waiting for transfers between devices: 174 us -> none
    add x3 -> x0, other arithmetic: 151 us -> none  [on_device(): carry = jnp.exp(decays_in[source])[:, None] * carry + states_in[source]]
    all_to_all x2 -> x4, starting transfers between devices: 21.5 us -> 40.3 us  [the longest x1 18.2 us: on_device(): lax.all_to_all(copies, 'grp', 0, 0, tiled=False).reshape(grp_count, -1)]
    all_to_all x2 -> x4, waiting for transfers between devices: 21.3 us -> 33.4 us  [the longest x1 21.1 us: on_device(): lax.all_to_all(copies, 'grp', 0, 0, tiled=False).reshape(grp_count, -1)]
    all_to_all x2 -> x0, local copies, waits for them, and re-layouts: 11.5 us -> none  [on_device(): arrived = lax.all_to_all(payload, 'seq', 0, 0, tiled=True)]
    ppermute x1, starting transfers between devices: 13.1 us -> 2.05 us  [on_device(): swapped = lax.ppermute(handoff, ('seq', 'grp'), swap)]
    unnamed x98 -> x124, local copies, waits for them, and re-layouts: 20.7 us -> 13.6 us
  transfers between devices with their start and end apart: 7 -> 8, of which waited for: 2 -> 4; matrix products, arithmetic and copies ran while one was open for 50% -> 41% of each run, Pallas kernels for 0% -> 0%
where the time goes in v2:
time: 225 us; the launch traced here: 221 us
  local copies, waits for them, and re-layouts  58.5 us (26%)
  starting transfers between devices  52.5 us (23%)
  other arithmetic  38.2 us (17%)
  waiting for transfers between devices  37.1 us (16%)
  matrix products  32.9 us (15%)
    all_to_all x1, waiting for transfers between devices, on_device(): lax.all_to_all(copies, 'grp', 0, 0, tiled=False).reshape(grp_count, -1)  21.1 us
    all_to_all x1, starting transfers between devices, on_device(): lax.all_to_all(copies, 'grp', 0, 0, tiled=False).reshape(grp_count, -1)  18.2 us
    all_to_all x2, starting transfers between devices, exchanged(): arrived = lax.all_to_all(packed, axis, 0, 0, tiled=False)  16 us
    unnamed x124, local copies, waits for them, and re-layouts  13.6 us
    all_to_all x2, waiting for transfers between devices, exchanged(): arrived = lax.all_to_all(packed, axis, 0, 0, tiled=False)  12.3 us
    dot_general x2, matrix products, span_pass(): jnp.einsum('kts,skp->tkp', weights * intersection[None], inputs, precisio...  11.5 us
    ppermute x3, starting transfers between devices, passed_along(): lax.ppermute(value, axis, [(source, source + steps) for source in range(f...  10.1 us
    all_to_all x1, starting transfers between devices, on_device(): returned = lax.all_to_all(entering, 'seq', 0, 0, tiled=False)  6.2 us
  transfers between devices with their start and end apart: 8, of which 4 were waited for; matrix products, arithmetic and copies ran while one was open for 41% of the time, Pallas kernels for 0%

profile of v2, /device:TPU:8, one launch (start us, length us, event | category | flops | bytes accessed | tf_op | source)
XLA Modules:
  0.0 220.8 jit_solution(17753112374985704384)
XLA Ops:
  1.5 3.5 %collective-permute-start = (f32[3,1024]{1,0:T(4,128)S(1)}, f32[3,1024]{1,0:T(4,128)S(1)}, u32[]{:S(2)}, u32[]{:S(2)}) collective-permute-start(f32[3,1024]{1,0:T(4,128)S(1)} %slice.453), channel_id=1, source_target_pairs={{0,16},{16,32},{32,48},{48,64},{64,80},{80,96},{96,112},{112,128},... | collective-permute-start | bytes 36872 | tf_op jit(solution)/shard_map/ppermute | solution.py:48
  6.0 3.2 %collective-permute-start.2 = (f32[3,256]{1,0:T(4,128)S(1)}, f32[3,256]{1,0:T(4,128)S(1)}, u32[]{:S(2)}, u32[]{:S(2)}) collective-permute-start(f32[3,256]{1,0:T(4,128)S(1)} %slice.467), channel_id=1, source_target_pairs={{0,16},{16,32},{32,48},{48,64},{64,80},{80,96},{96,112},{112,128},... | collective-permute-start | bytes 9224 | tf_op jit(solution)/shard_map/ppermute | solution.py:48
  11.6 3.5 %collective-permute-start.1 = (f32[3,256]{1,0:T(4,128)}, f32[3,256]{1,0:T(4,128)}, u32[]{:S(2)}, u32[]{:S(2)}) collective-permute-start(f32[3,256]{1,0:T(4,128)} %slice.461), channel_id=1, source_target_pairs={{0,16},{16,32},{32,48},{48,64},{64,80},{80,96},{96,112},{112,128},... | collective-permute-start | bytes 9224 | tf_op jit(solution)/shard_map/ppermute | solution.py:48
  30.1 4.6 %divide_multiply_fusion = f32[512,1024]{1,0:T(8,128)S(1)} fusion(f32[512,1024]{1,0:T(8,128)} %convert_element_type.44, f32[3,1024]{1,0:T(4,128)S(1)} %collective-permute-done, f32[1024]{0:T(1024)S(1)} %bitcast.372, f32[1024]{0:T(1024)S(1)} %bitcast.370, f32[1024]{0:T(1024)S(1)} %bitcast.371, f32[1024]{0:T(1024)S(1)} %bitcast.369), kind=kLoop, calls=%fused_computation.33 | loop fusion | flops 7340032 | bytes 4222976 | tf_op jit(solution)/shard_map/jit(silu)/mul | solution.py:57
  41.8 2.3 %reshape.1047 = f32[16,128,128]{2,1,0:T(8,128)} reshape(f32[16,64,256]{2,1,0:T(8,128)} %convolution_add_fusion) | data formatting | bytes 2097152 | tf_op jit(solution)/shard_map/reshape | solution.py:31
  44.1 2.3 %pad_maximum_fusion.1 = f32[16,132,128]{2,1,0:T(8,128)} fusion(f32[16,1,128]{2,1,0:T(1,128)S(1)} %bitcast.364, f32[16,2,128]{2,1,0:T(2,128)S(1)} %reshape.1051, f32[16,1,128]{2,1,0:T(1,128)S(1)} %bitcast.363, f32[16,128,128]{2,1,0:T(8,128)} %reshape.1047), kind=kLoop, calls=%fused_computation.57 | loop fusion | flops 811008 | bytes 2162688 | tf_op jit(solution)/shard_map/concatenate | solution.py:29
  46.4 7.8 %all-to-all-start = ((f32[16,132,128]{2,1,0:T(8,128)}), f32[16,132,128]{2,1,0:T(8,128)}, u32[]{:S(2)}, u32[]{:S(2)}) async-start(f32[16,132,128]{2,1,0:T(8,128)} %pad_maximum_fusion.1), calls=%async_computation | async-start | bytes 2228224 | tf_op jit(solution)/shard_map/all_to_all | solution.py:36
  54.1 3.1 %fusion.151 = (bf16[1,8,64,1024]{3,2,1,0:T(8,128)(2,1)}, bf16[1,8,64,1024]{3,2,1,0:T(8,128)(2,1)}) fusion(bf16[2,8,64,1024]{3,2,1,0:T(8,128)(2,1)} %param.28), kind=kLoop, calls=%fused_computation.272 | loop fusion | bytes 4194304 | tf_op jit(solution)/shard_map/slice | solution.py:198
  71.8 5.7 %all-to-all-done = f32[16,132,128]{2,1,0:T(8,128)} async-done(((f32[16,132,128]{2,1,0:T(8,128)}), f32[16,132,128]{2,1,0:T(8,128)}, u32[]{:S(2)}, u32[]{:S(2)}) %all-to-all-start) | async-done | bytes 1081376 | tf_op jit(solution)/shard_map/all_to_all | solution.py:36
  77.5 8.2 %all-to-all-start.3 = ((f32[16,66,128]{2,1,0:T(8,128)}), f32[16,66,128]{2,1,0:T(8,128)}, u32[]{:S(2)}, u32[]{:S(2)}) async-start(f32[16,66,128]{2,1,0:T(8,128)} %copy.328), calls=%async_computation.3 | async-start | bytes 1179648 | tf_op jit(solution)/shard_map/all_to_all | solution.py:36
  93.4 6.6 %all-to-all-done.3 = f32[16,66,128]{2,1,0:T(8,128)} async-done(((f32[16,66,128]{2,1,0:T(8,128)}), f32[16,66,128]{2,1,0:T(8,128)}, u32[]{:S(2)}, u32[]{:S(2)}) %all-to-all-start.3) | async-done | bytes 540704 | tf_op jit(solution)/shard_map/all_to_all | solution.py:36
  100.0 6.2 %all-to-all-start.1 = ((f32[16,128,128]{2,1,0:T(8,128)}), f32[16,128,128]{2,1,0:T(8,128)}, u32[]{:S(2)}, u32[]{:S(2)}) async-start(f32[16,128,128]{2,1,0:T(8,128)} %copy.305), calls=%async_computation.1 | async-start | bytes 2097152 | tf_op jit(solution)/shard_map/all_to_all | solution.py:245
  124.4 3.7 %collective-permute-done.3 = f32[131,128]{1,0:T(8,128)S(1)} collective-permute-done((f32[131,128]{1,0:T(8,128)S(1)}, f32[131,128]{1,0:T(8,128)S(1)}, u32[]{:S(2)}, u32[]{:S(2)}) %collective-permute-start.3) | collective-permute-done | bytes 67104 | tf_op jit(solution)/shard_map/ppermute | solution.py:257
  129.2 18.2 %all-to-all-start.2 = ((f32[16,131,128]{2,1,0:T(8,128)}), f32[16,131,128]{2,1,0:T(8,128)}, u32[]{:S(2)}, u32[]{:S(2)}) async-start(f32[16,131,128]{2,1,0:T(8,128)} %broadcast_in_dim.85), calls=%async_computation.2 | async-start | bytes 2228224 | tf_op jit(solution)/shard_map/all_to_all | solution.py:259
  154.9 2.5 %reshape.1056 = f32[16,64,256]{2,1,0:T(8,128)} reshape(f32[16,128,128]{2,1,0:T(8,128)} %all-to-all-done.1) | data formatting | bytes 2097152 | tf_op jit(solution)/shard_map/reshape.112
  157.4 21.1 %all-to-all-done.2 = f32[16,131,128]{2,1,0:T(8,128)} async-done(((f32[16,131,128]{2,1,0:T(8,128)}), f32[16,131,128]{2,1,0:T(8,128)}, u32[]{:S(2)}, u32[]{:S(2)}) %all-to-all-start.2) | async-done | bytes 1073184 | tf_op jit(solution)/shard_map/all_to_all | solution.py:259
  183.0 2.3 %slice.507 = f32[16,16384]{1,0:T(8,128)} slice(f32[16,16768]{1,0:T(8,128)} %bitcast.325), slice={[0:16], [0:16384]} | slice | bytes 2097152 | tf_op jit(solution)/shard_map/slice | solution.py:261
  191.3 2.6 %copy.365 = f32[2,8,64,256]{3,2,1,0:T(8,128)} copy(f32[2,8,64,256]{3,1,2,0:T(8,128)} %bitcast.326) | data formatting | bytes 2097152
  195.5 2.2 convolution_bitcast_fusion.2
  199.3 6.5 %fusion.41 = f32[256,16,64]{0,2,1:T(8,128)S(1)} fusion(f32[1,256,16,64]{1,3,2,0:T(8,128)} %fusion.36, f32[256,256]{1,0:T(8,128)S(1)} %copy-done.16, f32[16,256]{1,0:T(8,128)S(1)} %copy-done.44, pred[256,256]{1,0:T(8,128)(4,1)S(1)} %copy-done.36, f32[1,512,16,64]{1,3,2,0:T(8,128)} %copy-done.1), kind=kOutput, calls=%fused_computation.46 | convolution fusion | flops 809762816 | bytes 3506176 | tf_op jit(solution)/shard_map/vmap(kts,skp->tkp)/dot_general | solution.py:83
  205.8 5.0 %fusion.47 = f32[256,16,64]{0,2,1:T(8,128)S(1)} fusion(f32[1,256,16,64]{1,3,2,0:T(8,128)S(1)} %fusion.37, f32[256,256]{1,0:T(8,128)S(1)} %copy-done.15, f32[16,256]{1,0:T(8,128)S(1)} %copy-done.45, pred[256,256]{1,0:T(8,128)(4,1)S(1)} %copy-done.36, f32[1,512,16,64]{1,3,2,0:T(8,128)S(1)} %copy-done.2), kind=kOutput, calls=%fused_computation.48 | convolution fusion | flops 809762816 | bytes 3506176 | tf_op jit(solution)/shard_map/vmap(kts,skp->tkp)/dot_general | solution.py:83
  210.9 3.3 %maximum_add_fusion = f32[512,16,64]{0,2,1:T(8,128)} fusion(f32[256,16,64]{0,2,1:T(8,128)S(1)} %fusion.41, f32[256,16,64]{0,2,1:T(8,128)S(1)} %fusion.47, f32[16,64,256]{2,1,0:T(8,128)S(1)} %copy-done.9, f32[512,16]{0,1:T(8,128)S(1)} %bitcast.342, f32[512,256]{1,0:T(8,128)S(1)} %copy-done.4), kind=kOutput, calls=%fused_computation.23 | convolution fusion | flops 1612185600 | bytes 5799936 | tf_op jit(solution)/shard_map/gsn,gkpn->gskp/dot_general | solution.py:277
  214.2 2.9 %copy.306 = f32[512,1024]{1,0:T(8,128)} copy(f32[512,1024]{0,1:T(8,128)} %bitcast.318) | data formatting | bytes 4194304 | tf_op jit(solution)/shard_map/reshape;transpose | solution.py:281
  217.7 3.1 %add_convert_fusion = bf16[512,1024]{1,0:T(8,128)(2,1)} fusion(f32[512,1024]{1,0:T(8,128)} %copy.306, f32[512,1024]{1,0:T(8,128)S(1)} %divide_multiply_fusion, f32[1024]{0:T(1024)S(1)} %copy-done.46), kind=kLoop, calls=%fused_computation.24 | loop fusion | flops 1572864 | bytes 5246976 | tf_op jit(solution)/shard_map/convert_element_type | solution.py:284
  (289 shorter events, 88.9 us)
Async XLA Ops:
  0.6 59.6 %copy-start = (bf16[2,8,8192]{2,1,0:T(8,128)(2,1)S(1)}, bf16[2,8,8192]{2,1,0:T(8,128)(2,1)}, u32[]{:S(2)}) copy-start(bf16[2,8,8192]{2,1,0:T(8,128)(2,1)} %param.26) | copy-start | bytes 786436
  0.6 26.5 %copy-start.13 = (bf16[512,1024]{1,0:T(8,128)(2,1)S(1)}, bf16[512,1024]{1,0:T(8,128)(2,1)}, u32[]{:S(2)}) copy-start(bf16[512,1024]{1,0:T(8,128)(2,1)} %param.15) | copy-start | bytes 3145732
  1.5 28.7 %collective-permute-start = (f32[3,1024]{1,0:T(4,128)S(1)}, f32[3,1024]{1,0:T(4,128)S(1)}, u32[]{:S(2)}, u32[]{:S(2)}) collective-permute-start(f32[3,1024]{1,0:T(4,128)S(1)} %slice.453), channel_id=1, source_target_pairs={{0,16},{16,32},{32,48},{48,64},{64,80},{80,96},{96,112},{112,128},... | collective-permute-start | bytes 36872 | tf_op jit(solution)/shard_map/ppermute | solution.py:48
  6.0 23.0 %collective-permute-start.2 = (f32[3,256]{1,0:T(4,128)S(1)}, f32[3,256]{1,0:T(4,128)S(1)}, u32[]{:S(2)}, u32[]{:S(2)}) collective-permute-start(f32[3,256]{1,0:T(4,128)S(1)} %slice.467), channel_id=1, source_target_pairs={{0,16},{16,32},{32,48},{48,64},{64,80},{80,96},{96,112},{112,128},... | collective-permute-start | bytes 9224 | tf_op jit(solution)/shard_map/ppermute | solution.py:48
  11.6 173.7 %collective-permute-start.1 = (f32[3,256]{1,0:T(4,128)}, f32[3,256]{1,0:T(4,128)}, u32[]{:S(2)}, u32[]{:S(2)}) collective-permute-start(f32[3,256]{1,0:T(4,128)} %slice.461), channel_id=1, source_target_pairs={{0,16},{16,32},{32,48},{48,64},{64,80},{80,96},{96,112},{112,128},... | collective-permute-start | bytes 9224 | tf_op jit(solution)/shard_map/ppermute | solution.py:48
  46.4 31.1 %all-to-all-start = ((f32[16,132,128]{2,1,0:T(8,128)}), f32[16,132,128]{2,1,0:T(8,128)}, u32[]{:S(2)}, u32[]{:S(2)}) async-start(f32[16,132,128]{2,1,0:T(8,128)} %pad_maximum_fusion.1), calls=%async_computation | async-start | bytes 2228224 | tf_op jit(solution)/shard_map/all_to_all | solution.py:36
  77.5 22.5 %all-to-all-start.3 = ((f32[16,66,128]{2,1,0:T(8,128)}), f32[16,66,128]{2,1,0:T(8,128)}, u32[]{:S(2)}, u32[]{:S(2)}) async-start(f32[16,66,128]{2,1,0:T(8,128)} %copy.328), calls=%async_computation.3 | async-start | bytes 1179648 | tf_op jit(solution)/shard_map/all_to_all | solution.py:36
  92.0 14.2 %copy-start.42 = (f32[2,8,16]{2,1,0:T(8,128)S(1)}, f32[2,8,16]{2,1,0:T(8,128)}, u32[]{:S(2)}) copy-start(f32[2,8,16]{2,1,0:T(8,128)} %param.25) | copy-start | bytes 3076
  92.0 14.2 %copy-start.51 = (f32[16]{0:T(128)S(1)}, f32[16]{0:T(128)}, u32[]{:S(2)}) copy-start(f32[16]{0:T(128)} %get-tuple-element.79) | copy-start | bytes 196
  92.0 14.8 %copy-start.20 = (f32[1,16,2,128]{3,1,2,0:T(8,128)S(1)}, f32[1,16,2,128]{3,1,2,0:T(8,128)}, u32[]{:S(2)}) copy-start(f32[1,16,2,128]{3,1,2,0:T(8,128)} %copy-done.19) | copy-start | bytes 49156
  92.0 16.1 %copy-start.50 = (f32[16]{0:T(128)S(1)}, f32[16]{0:T(128)}, u32[]{:S(2)}) copy-start(f32[16]{0:T(128)} %get-tuple-element.73) | copy-start | bytes 196
  92.1 16.8 %copy-start.29 = (f32[16,4,128]{2,0,1:T(8,128)S(1)}, f32[16,4,128]{2,0,1:T(8,128)}, u32[]{:S(2)}) copy-start(f32[16,4,128]{2,0,1:T(8,128)} %get-tuple-element.60) | copy-start | bytes 98308
  92.1 18.7 %copy-start.37 = (f32[1,256,16]{1,0,2:T(1,128)S(1)}, f32[1,256,16]{1,0,2:T(1,128)}, u32[]{:S(2)}) copy-start(f32[1,256,16]{1,0,2:T(1,128)} %get-tuple-element.25) | copy-start | bytes 49156
  92.1 19.3 %copy-start.30 = (bf16[2,8,1024]{2,1,0:T(8,128)(2,1)S(1)}, bf16[2,8,1024]{2,1,0:T(8,128)(2,1)}, u32[]{:S(2)}) copy-start(bf16[2,8,1024]{2,1,0:T(8,128)(2,1)} %param.22) | copy-start | bytes 98308
  100.0 28.1 %all-to-all-start.1 = ((f32[16,128,128]{2,1,0:T(8,128)}), f32[16,128,128]{2,1,0:T(8,128)}, u32[]{:S(2)}, u32[]{:S(2)}) async-start(f32[16,128,128]{2,1,0:T(8,128)} %copy.305), calls=%async_computation.1 | async-start | bytes 2097152 | tf_op jit(solution)/shard_map/all_to_all | solution.py:245
  122.3 25.1 %copy-start.24 = (f32[16,2,128]{2,1,0:T(2,128)S(1)}, f32[16,2,128]{2,1,0:T(2,128)}, u32[]{:S(2)}) copy-start(f32[16,2,128]{2,1,0:T(2,128)} %copy-done.23) | copy-start | bytes 49156
  122.3 25.7 %copy-start.31 = (bf16[2,8,8,128]{3,1,2,0:T(8,128)(2,1)S(1)}, bf16[2,8,8,128]{3,1,2,0:T(8,128)(2,1)}, u32[]{:S(2)}) copy-start(bf16[2,8,8,128]{3,1,2,0:T(8,128)(2,1)} %get-tuple-element.58) | copy-start | bytes 98308
  122.3 28.3 %copy-start.22 = (f32[2,8,64,2]{2,1,3,0:T(8,128)S(1)}, f32[2,8,64,2]{2,1,3,0:T(8,128)}, u32[]{:S(2)}) copy-start(f32[2,8,64,2]{2,1,3,0:T(8,128)} %copy-done.21) | copy-start | bytes 24580
  122.4 5.8 %collective-permute-start.3 = (f32[131,128]{1,0:T(8,128)S(1)}, f32[131,128]{1,0:T(8,128)S(1)}, u32[]{:S(2)}, u32[]{:S(2)}) collective-permute-start(f32[131,128]{1,0:T(8,128)S(1)} %pad_bitcast_fusion), channel_id=1, source_target_pairs={{0,0},{1,16},{2,32},{3,48},{4,64},{5,80},{6,96},{7,112},{8,128},{9... | collective-permute-start | bytes 201224 | tf_op jit(solution)/shard_map/ppermute | solution.py:257
  129.2 18.2 %copy-start.35 = (f32[1,16,2,128]{3,2,1,0:T(2,128)S(1)}, f32[1,16,2,128]{3,2,1,0:T(2,128)}, u32[]{:S(2)}) copy-start(f32[1,16,2,128]{3,2,1,0:T(2,128)} %copy.292) | copy-start | bytes 49156
  129.2 49.3 %all-to-all-start.2 = ((f32[16,131,128]{2,1,0:T(8,128)}), f32[16,131,128]{2,1,0:T(8,128)}, u32[]{:S(2)}, u32[]{:S(2)}) async-start(f32[16,131,128]{2,1,0:T(8,128)} %broadcast_in_dim.85), calls=%async_computation.2 | async-start | bytes 2228224 | tf_op jit(solution)/shard_map/all_to_all | solution.py:259
  190.7 7.1 %copy-start.18 = (f32[1,8,16,64]{3,2,1,0:T(8,128)S(1)}, f32[1,8,16,64]{3,2,1,0:T(8,128)}, u32[]{:S(2)}) copy-start(f32[1,8,16,64]{3,2,1,0:T(8,128)} %squeeze.24) | copy-start | bytes 98308
  190.7 7.1 %copy-start.41 = (f32[8,16]{0,1:T(8,128)S(1)}, f32[8,16]{0,1:T(8,128)}, u32[]{:S(2)}) copy-start(f32[8,16]{0,1:T(8,128)} %copy.309) | copy-start | bytes 1540
  190.7 7.1 %copy-start.49 = (f32[16]{0:T(128)S(1)}, f32[16]{0:T(128)}, u32[]{:S(2)}) copy-start(f32[16]{0:T(128)} %get-tuple-element.72) | copy-start | bytes 196
  (40 other events, 147.7 us)

commit v3 on v2

--- a/solution.py
+++ b/solution.py
@@ -247,28 +247,43 @@
 
     state_size = chunk_heads * HDIM * STATE
     tail_size = tail_x_parts.shape[1]
+    bc_size = tail_bc_in.shape[1]
+
+    def whole_rows(value):
+        return jnp.pad(value, (0, -value.shape[0] % LANES)).reshape(-1, LANES)
+
     handoff = jnp.concatenate(
-        [carry.reshape(-1), tail_x_in[seq_count - 1], tail_bc_in[seq_count - 1]], axis=0
-    )
-    handoff = jnp.pad(handoff, (0, -handoff.shape[0] % LANES)).reshape(-1, LANES)
+        [
+            whole_rows(carry.reshape(-1)),
+            whole_rows(tail_x_in[seq_count - 1]),
+            whole_rows(tail_bc_in[seq_count - 1]),
+        ],
+        axis=0,
+    )
     swap = [
         (a * grp_count + b, b * grp_count + a) for a in range(seq_count) for b in range(grp_count)
     ]
     swapped = lax.ppermute(handoff, ("seq", "grp"), swap)
     copies = jnp.broadcast_to(swapped[None], (grp_count,) + swapped.shape)
-    gathered = lax.all_to_all(copies, "grp", 0, 0, tiled=False).reshape(grp_count, -1)
+    gathered = lax.all_to_all(copies, "grp", 0, 0, tiled=False)
+    state_rows = -(-state_size // LANES)
+    tail_rows_count = -(-tail_size // LANES)
     state_heads = HEADS // seq_count
-    prefix_state = gathered[:, :state_size].reshape(state_heads, HDIM, STATE)
+    prefix_state = (
+        gathered[:, :state_rows].reshape(grp_count, -1)[:, :state_size].reshape(state_heads, HDIM, STATE)
+    )
     prefix_tail = (
-        gathered[:, state_size : state_size + tail_size]
+        gathered[:, state_rows : state_rows + tail_rows_count]
+        .reshape(grp_count, -1)[:, :tail_size]
         .reshape(grp_count, edge, chunk_heads * HDIM)
         .transpose(1, 0, 2)
         .reshape(edge, state_heads * HDIM)
     )
     dgroup_width = tail_rows[1].shape[1]
-    bc_size = 2 * edge * dgroup_width // grp_count
-    tail_bc_all = gathered[:, state_size + tail_size : state_size + tail_size + bc_size].reshape(
-        2 * edge, dgroup_width
+    tail_bc_all = (
+        gathered[:, state_rows + tail_rows_count :]
+        .reshape(grp_count, -1)[:, :bc_size]
+        .reshape(2 * edge, dgroup_width)
     )
     tail_b = tail_bc_all[:edge]
     tail_c = tail_bc_all[edge:]

time: 225 us -> 228 us (1.013)
  waiting for transfers between devices: 37.1 us -> 43.5 us
  local copies, waits for them, and re-layouts: 58.5 us -> 55.9 us
    unnamed x124 -> x111, local copies, waits for them, and re-layouts: 13.6 us -> 7.36 us
    all_to_all x2, waiting for transfers between devices: 12.3 us -> 16.4 us  [exchanged(): arrived = lax.all_to_all(packed, axis, 0, 0, tiled=False)]
    another operation x19 -> x20, local copies, waits for them, and re-layouts: 4.43 us -> 6.99 us
  transfers between devices with their start and end apart: 8 -> 8, of which waited for: 4 -> 5; matrix products, arithmetic and copies ran while one was open for 41% -> 37% of each run, Pallas kernels for 0% -> 0%
where the time goes in v3:
time: 228 us; the launch traced here: 224 us
  local copies, waits for them, and re-layouts  55.9 us (25%)
  starting transfers between devices  52.2 us (23%)
  waiting for transfers between devices  43.5 us (19%)
  other arithmetic  36 us (16%)
  matrix products  34.8 us (15%)
    all_to_all x1, waiting for transfers between devices, on_device(): gathered = lax.all_to_all(copies, 'grp', 0, 0, tiled=False)  23.2 us
    all_to_all x1, starting transfers between devices, on_device(): gathered = lax.all_to_all(copies, 'grp', 0, 0, tiled=False)  18 us
    all_to_all x2, waiting for transfers between devices, exchanged(): arrived = lax.all_to_all(packed, axis, 0, 0, tiled=False)  16.4 us
    all_to_all x2, starting transfers between devices, exchanged(): arrived = lax.all_to_all(packed, axis, 0, 0, tiled=False)  16 us
    dot_general x2, matrix products, span_pass(): jnp.einsum('kts,skp->tkp', weights * intersection[None], inputs, precisio...  11.5 us
    ppermute x3, starting transfers between devices, passed_along(): lax.ppermute(value, axis, [(source, source + steps) for source in range(f...  10.1 us
    unnamed x111, local copies, waits for them, and re-layouts  7.36 us
    all_to_all x1, starting transfers between devices, on_device(): returned = lax.all_to_all(entering, 'seq', 0, 0, tiled=False)  6.2 us
  transfers between devices with their start and end apart: 8, of which 5 were waited for; matrix products, arithmetic and copies ran while one was open for 37% of the time, Pallas kernels for 0%

profile of v3, /device:TPU:8, one launch (start us, length us, event | category | flops | bytes accessed | tf_op | source)
XLA Modules:
  0.0 224.0 jit_solution(1342492630465777160)
XLA Ops:
  1.4 3.5 %collective-permute-start = (f32[3,1024]{1,0:T(4,128)S(1)}, f32[3,1024]{1,0:T(4,128)S(1)}, u32[]{:S(2)}, u32[]{:S(2)}) collective-permute-start(f32[3,1024]{1,0:T(4,128)S(1)} %slice.461), channel_id=1, source_target_pairs={{0,16},{16,32},{32,48},{48,64},{64,80},{80,96},{96,112},{112,128},... | collective-permute-start | bytes 36872 | tf_op jit(solution)/shard_map/ppermute | solution.py:48
  5.9 3.2 %collective-permute-start.2 = (f32[3,256]{1,0:T(4,128)S(1)}, f32[3,256]{1,0:T(4,128)S(1)}, u32[]{:S(2)}, u32[]{:S(2)}) collective-permute-start(f32[3,256]{1,0:T(4,128)S(1)} %slice.475), channel_id=1, source_target_pairs={{0,16},{16,32},{32,48},{48,64},{64,80},{80,96},{96,112},{112,128},... | collective-permute-start | bytes 9224 | tf_op jit(solution)/shard_map/ppermute | solution.py:48
  11.5 3.5 %collective-permute-start.1 = (f32[3,256]{1,0:T(4,128)}, f32[3,256]{1,0:T(4,128)}, u32[]{:S(2)}, u32[]{:S(2)}) collective-permute-start(f32[3,256]{1,0:T(4,128)} %slice.469), channel_id=1, source_target_pairs={{0,16},{16,32},{32,48},{48,64},{64,80},{80,96},{96,112},{112,128},... | collective-permute-start | bytes 9224 | tf_op jit(solution)/shard_map/ppermute | solution.py:48
  43.4 2.3 %reshape.1054 = f32[16,128,128]{2,1,0:T(8,128)} reshape(f32[16,64,256]{2,1,0:T(8,128)} %convolution_add_fusion) | data formatting | bytes 2097152 | tf_op jit(solution)/shard_map/reshape | solution.py:31
  45.7 2.3 %pad_maximum_fusion.1 = f32[16,132,128]{2,1,0:T(8,128)} fusion(f32[16,1,128]{2,1,0:T(1,128)S(1)} %bitcast.359, f32[16,2,128]{2,1,0:T(2,128)S(1)} %reshape.1058, f32[16,1,128]{2,1,0:T(1,128)S(1)} %bitcast.358, f32[16,128,128]{2,1,0:T(8,128)} %reshape.1054), kind=kLoop, calls=%fused_computation.57 | loop fusion | flops 811008 | bytes 2162688 | tf_op jit(solution)/shard_map/concatenate | solution.py:29
  48.0 7.8 %all-to-all-start = ((f32[16,132,128]{2,1,0:T(8,128)}), f32[16,132,128]{2,1,0:T(8,128)}, u32[]{:S(2)}, u32[]{:S(2)}) async-start(f32[16,132,128]{2,1,0:T(8,128)} %pad_maximum_fusion.1), calls=%async_computation | async-start | bytes 2228224 | tf_op jit(solution)/shard_map/all_to_all | solution.py:36
  55.9 2.7 %fusion.158 = (f32[2,8,8,8]{3,0,2,1:T(2,128)S(1)}, f32[2,8,8,8,64]{4,3,0,2,1:T(8,128)}) fusion(bf16[2,8,8,8,128]{4,1,3,2,0:T(8,128)(2,1)S(1)} %bitcast.315, bf16[8,64,8,128,1]{3,2,1,0,4:T(8,128)(2,1)} %bitcast_bitcast_fusion.1, pred[8,64]{1,0:T(8,128)(4,1)S(1)} %broadcast_compare_fusion), kind=kOutput, calls=%fused_computation.281 | convolution fusion | flops 16972800 | bytes 1577472 | tf_op jit(solution)/shard_map/jrkgd,rckd->jrkgc/dot_general | solution.py:201
  69.3 9.8 %all-to-all-done = f32[16,132,128]{2,1,0:T(8,128)} async-done(((f32[16,132,128]{2,1,0:T(8,128)}), f32[16,132,128]{2,1,0:T(8,128)}, u32[]{:S(2)}, u32[]{:S(2)}) %all-to-all-start) | async-done | bytes 1081376 | tf_op jit(solution)/shard_map/all_to_all | solution.py:36
  79.1 8.2 %all-to-all-start.3 = ((f32[16,66,128]{2,1,0:T(8,128)}), f32[16,66,128]{2,1,0:T(8,128)}, u32[]{:S(2)}, u32[]{:S(2)}) async-start(f32[16,66,128]{2,1,0:T(8,128)} %copy.327), calls=%async_computation.3 | async-start | bytes 1179648 | tf_op jit(solution)/shard_map/all_to_all | solution.py:36
  95.0 6.6 %all-to-all-done.3 = f32[16,66,128]{2,1,0:T(8,128)} async-done(((f32[16,66,128]{2,1,0:T(8,128)}), f32[16,66,128]{2,1,0:T(8,128)}, u32[]{:S(2)}, u32[]{:S(2)}) %all-to-all-start.3) | async-done | bytes 540704 | tf_op jit(solution)/shard_map/all_to_all | solution.py:36
  101.6 6.2 %all-to-all-start.1 = ((f32[16,128,128]{2,1,0:T(8,128)}), f32[16,128,128]{2,1,0:T(8,128)}, u32[]{:S(2)}, u32[]{:S(2)}) async-start(f32[16,128,128]{2,1,0:T(8,128)} %copy.304), calls=%async_computation.1 | async-start | bytes 2097152 | tf_op jit(solution)/shard_map/all_to_all | solution.py:245
  125.9 3.7 %collective-permute-done.3 = f32[131,128]{1,0:T(8,128)S(1)} collective-permute-done((f32[131,128]{1,0:T(8,128)S(1)}, f32[131,128]{1,0:T(8,128)S(1)}, u32[]{:S(2)}, u32[]{:S(2)}) %collective-permute-start.3) | collective-permute-done | bytes 67104 | tf_op jit(solution)/shard_map/ppermute | solution.py:266
  130.8 18.0 %all-to-all-start.2 = ((f32[16,131,128]{2,1,0:T(8,128)}), f32[16,131,128]{2,1,0:T(8,128)}, u32[]{:S(2)}, u32[]{:S(2)}) async-start(f32[16,131,128]{2,1,0:T(8,128)} %broadcast_in_dim.85), calls=%async_computation.2 | async-start | bytes 2228224 | tf_op jit(solution)/shard_map/all_to_all | solution.py:268
  154.3 2.5 %reshape.1063 = f32[16,64,256]{2,1,0:T(8,128)} reshape(f32[16,128,128]{2,1,0:T(8,128)} %all-to-all-done.1) | data formatting | bytes 2097152 | tf_op jit(solution)/shard_map/reshape.114
  156.8 23.2 %all-to-all-done.2 = f32[16,131,128]{2,1,0:T(8,128)} async-done(((f32[16,131,128]{2,1,0:T(8,128)}), f32[16,131,128]{2,1,0:T(8,128)}, u32[]{:S(2)}, u32[]{:S(2)}) %all-to-all-start.2) | async-done | bytes 1073184 | tf_op jit(solution)/shard_map/all_to_all | solution.py:268
  184.3 2.3 %fusion.93 = f32[256,256]{1,0:T(8,128)} fusion(f32[1,512,256]{2,1,0:T(8,128)} %multiply_bitcast_fusion, f32[1,512,256]{2,1,0:T(8,128)S(1)} %bitcast.319), kind=kOutput, calls=%fused_computation.113 | convolution fusion | flops 201326592 | bytes 786432 | tf_op jit(solution)/shard_map/vmap()/dot_general | solution.py:82
  191.2 2.3 %slice.517 = f32[16,128,128]{2,1,0:T(8,128)} slice(f32[16,131,128]{2,1,0:T(8,128)} %all-to-all-done.2), slice={[0:16], [0:128], [0:128]} | slice | bytes 2097152 | tf_op jit(solution)/shard_map/slice | solution.py:273
  193.6 2.6 %reshape_reshape.2 = f32[16,64,256]{2,1,0:T(8,128)} reshape(f32[16,128,128]{2,1,0:T(8,128)} %slice.517) | data formatting | bytes 2097152 | tf_op jit(solution)/shard_map/reshape;reshape | solution.py:273
  198.7 2.2 convolution_bitcast_fusion.2
  202.5 6.5 %fusion.41 = f32[256,16,64]{0,2,1:T(8,128)S(1)} fusion(f32[1,256,16,64]{1,3,2,0:T(8,128)} %fusion.36, f32[256,256]{1,0:T(8,128)S(1)} %copy-done.13, f32[16,256]{1,0:T(8,128)S(1)} %copy-done.39, pred[256,256]{1,0:T(8,128)(4,1)S(1)} %copy-done.31, f32[1,512,16,64]{1,3,2,0:T(8,128)} %copy-done.1), kind=kOutput, calls=%fused_computation.46 | convolution fusion | flops 809762816 | bytes 3506176 | tf_op jit(solution)/shard_map/vmap(kts,skp->tkp)/dot_general | solution.py:83
  209.0 5.0 %fusion.47 = f32[256,16,64]{0,2,1:T(8,128)S(1)} fusion(f32[1,256,16,64]{1,3,2,0:T(8,128)S(1)} %fusion.37, f32[256,256]{1,0:T(8,128)S(1)} %copy-done.12, f32[16,256]{1,0:T(8,128)S(1)} %copy-done.38, pred[256,256]{1,0:T(8,128)(4,1)S(1)} %copy-done.31, f32[1,512,16,64]{1,3,2,0:T(8,128)S(1)} %copy-done.2), kind=kOutput, calls=%fused_computation.48 | convolution fusion | flops 809762816 | bytes 3506176 | tf_op jit(solution)/shard_map/vmap(kts,skp->tkp)/dot_general | solution.py:83
  214.1 3.3 %maximum_add_fusion = f32[512,16,64]{0,2,1:T(8,128)} fusion(f32[256,16,64]{0,2,1:T(8,128)S(1)} %fusion.41, f32[256,16,64]{0,2,1:T(8,128)S(1)} %fusion.47, f32[16,64,256]{2,1,0:T(8,128)S(1)} %copy-done.8, f32[512,16]{0,1:T(8,128)S(1)} %bitcast.337, f32[512,256]{1,0:T(8,128)S(1)} %copy-done.5), kind=kOutput, calls=%fused_computation.23 | convolution fusion | flops 1612185600 | bytes 5799936 | tf_op jit(solution)/shard_map/gsn,gkpn->gskp/dot_general | solution.py:292
  217.4 2.9 %copy.305 = f32[512,1024]{1,0:T(8,128)} copy(f32[512,1024]{0,1:T(8,128)} %bitcast.318) | data formatting | bytes 4194304 | tf_op jit(solution)/shard_map/reshape;transpose | solution.py:296
  221.0 3.1 %add_convert_fusion = bf16[512,1024]{1,0:T(8,128)(2,1)} fusion(f32[512,1024]{1,0:T(8,128)} %copy.305, f32[512,1024]{1,0:T(8,128)S(1)} %divide_multiply_fusion, f32[1024]{0:T(1024)S(1)} %copy-done.40), kind=kLoop, calls=%fused_computation.24 | loop fusion | flops 1572864 | bytes 5246976 | tf_op jit(solution)/shard_map/convert_element_type | solution.py:299
  (279 shorter events, 88.8 us)
Async XLA Ops:
  0.6 55.2 %copy-start = (bf16[2,8,8192]{2,1,0:T(8,128)(2,1)S(1)}, bf16[2,8,8192]{2,1,0:T(8,128)(2,1)}, u32[]{:S(2)}) copy-start(bf16[2,8,8192]{2,1,0:T(8,128)(2,1)} %param.26) | copy-start | bytes 786436
  1.4 33.6 %collective-permute-start = (f32[3,1024]{1,0:T(4,128)S(1)}, f32[3,1024]{1,0:T(4,128)S(1)}, u32[]{:S(2)}, u32[]{:S(2)}) collective-permute-start(f32[3,1024]{1,0:T(4,128)S(1)} %slice.461), channel_id=1, source_target_pairs={{0,16},{16,32},{32,48},{48,64},{64,80},{80,96},{96,112},{112,128},... | collective-permute-start | bytes 36872 | tf_op jit(solution)/shard_map/ppermute | solution.py:48
  5.9 28.0 %collective-permute-start.2 = (f32[3,256]{1,0:T(4,128)S(1)}, f32[3,256]{1,0:T(4,128)S(1)}, u32[]{:S(2)}, u32[]{:S(2)}) collective-permute-start(f32[3,256]{1,0:T(4,128)S(1)} %slice.475), channel_id=1, source_target_pairs={{0,16},{16,32},{32,48},{48,64},{64,80},{80,96},{96,112},{112,128},... | collective-permute-start | bytes 9224 | tf_op jit(solution)/shard_map/ppermute | solution.py:48
  11.5 170.6 %collective-permute-start.1 = (f32[3,256]{1,0:T(4,128)}, f32[3,256]{1,0:T(4,128)}, u32[]{:S(2)}, u32[]{:S(2)}) collective-permute-start(f32[3,256]{1,0:T(4,128)} %slice.469), channel_id=1, source_target_pairs={{0,16},{16,32},{32,48},{48,64},{64,80},{80,96},{96,112},{112,128},... | collective-permute-start | bytes 9224 | tf_op jit(solution)/shard_map/ppermute | solution.py:48
  18.2 9.9 %copy-start.18 = (f32[16,2,128]{2,1,0:T(2,128)}, f32[16,2,128]{2,1,0:T(2,128)S(1)}, u32[]{:S(2)}) copy-start(f32[16,2,128]{2,1,0:T(2,128)S(1)} %broadcast.557) | copy-start | bytes 49156
  45.7 10.1 %copy-start.47 = (s32[8]{0:T(128)S(1)}, s32[8]{0:T(128)}, u32[]{:S(2)}) copy-start(s32[8]{0:T(128)} %param.29) | copy-start | bytes 100
  45.7 10.1 %copy-start.48 = (s32[64]{0:T(128)S(1)}, s32[64]{0:T(128)}, u32[]{:S(2)}) copy-start(s32[64]{0:T(128)} %iota_add_fusion) | copy-start | bytes 772
  48.0 31.1 %all-to-all-start = ((f32[16,132,128]{2,1,0:T(8,128)}), f32[16,132,128]{2,1,0:T(8,128)}, u32[]{:S(2)}, u32[]{:S(2)}) async-start(f32[16,132,128]{2,1,0:T(8,128)} %pad_maximum_fusion.1), calls=%async_computation | async-start | bytes 2228224 | tf_op jit(solution)/shard_map/all_to_all | solution.py:36
  69.3 23.1 %copy-start.34 = (f32[2,8,16]{2,1,0:T(8,128)}, f32[2,8,16]{2,1,0:T(8,128)S(1)}, u32[]{:S(2)}) copy-start(f32[2,8,16]{2,1,0:T(8,128)S(1)} %multiply_exponential_fusion) | copy-start | bytes 3076
  79.1 22.5 %all-to-all-start.3 = ((f32[16,66,128]{2,1,0:T(8,128)}), f32[16,66,128]{2,1,0:T(8,128)}, u32[]{:S(2)}, u32[]{:S(2)}) async-start(f32[16,66,128]{2,1,0:T(8,128)} %copy.327), calls=%async_computation.3 | async-start | bytes 1179648 | tf_op jit(solution)/shard_map/all_to_all | solution.py:36
  93.7 14.2 %copy-start.44 = (f32[256]{0:T(256)S(1)}, f32[256]{0:T(256)}, u32[]{:S(2)}) copy-start(f32[256]{0:T(256)} %param.20) | copy-start | bytes 3076
  93.7 15.4 %copy-start.17 = (f32[1,16,2,128]{3,1,2,0:T(8,128)S(1)}, f32[1,16,2,128]{3,1,2,0:T(8,128)}, u32[]{:S(2)}) copy-start(f32[1,16,2,128]{3,1,2,0:T(8,128)} %copy-done.16) | copy-start | bytes 49156
  93.7 17.4 %copy-start.24 = (f32[16,4,128]{2,0,1:T(8,128)S(1)}, f32[16,4,128]{2,0,1:T(8,128)}, u32[]{:S(2)}) copy-start(f32[16,4,128]{2,0,1:T(8,128)} %get-tuple-element.58) | copy-start | bytes 98308
  93.7 18.0 %copy-start.32 = (f32[1,256,16]{1,0,2:T(1,128)S(1)}, f32[1,256,16]{1,0,2:T(1,128)}, u32[]{:S(2)}) copy-start(f32[1,256,16]{1,0,2:T(1,128)} %get-tuple-element.25) | copy-start | bytes 49156
  93.7 19.9 %copy-start.25 = (bf16[2,8,1024]{2,1,0:T(8,128)(2,1)S(1)}, bf16[2,8,1024]{2,1,0:T(8,128)(2,1)}, u32[]{:S(2)}) copy-start(bf16[2,8,1024]{2,1,0:T(8,128)(2,1)} %param.22) | copy-start | bytes 98308
  101.6 28.1 %all-to-all-start.1 = ((f32[16,128,128]{2,1,0:T(8,128)}), f32[16,128,128]{2,1,0:T(8,128)}, u32[]{:S(2)}, u32[]{:S(2)}) async-start(f32[16,128,128]{2,1,0:T(8,128)} %copy.304), calls=%async_computation.1 | async-start | bytes 2097152 | tf_op jit(solution)/shard_map/all_to_all | solution.py:245
  117.9 31.0 %copy-start.20 = (f32[16,2,128]{2,1,0:T(2,128)S(1)}, f32[16,2,128]{2,1,0:T(2,128)}, u32[]{:S(2)}) copy-start(f32[16,2,128]{2,1,0:T(2,128)} %copy-done.19) | copy-start | bytes 49156
  117.9 31.6 %copy-start.26 = (bf16[2,8,8,128]{3,1,2,0:T(8,128)(2,1)S(1)}, bf16[2,8,8,128]{3,1,2,0:T(8,128)(2,1)}, u32[]{:S(2)}) copy-start(bf16[2,8,8,128]{3,1,2,0:T(8,128)(2,1)} %get-tuple-element.56) | copy-start | bytes 98308
  123.9 5.6 %collective-permute-start.3 = (f32[131,128]{1,0:T(8,128)S(1)}, f32[131,128]{1,0:T(8,128)S(1)}, u32[]{:S(2)}, u32[]{:S(2)}) collective-permute-start(f32[131,128]{1,0:T(8,128)S(1)} %pad_maximum_fusion.5), channel_id=1, source_target_pairs={{0,0},{1,16},{2,32},{3,48},{4,64},{5,80},{6,96},{7,112},{8,128},{9... | collective-permute-start | bytes 201224 | tf_op jit(solution)/shard_map/ppermute | solution.py:266
  130.8 18.0 %copy-start.30 = (f32[1,16,2,128]{3,2,1,0:T(2,128)S(1)}, f32[1,16,2,128]{3,2,1,0:T(2,128)}, u32[]{:S(2)}) copy-start(f32[1,16,2,128]{3,2,1,0:T(2,128)} %copy.295) | copy-start | bytes 49156
  130.8 49.2 %all-to-all-start.2 = ((f32[16,131,128]{2,1,0:T(8,128)}), f32[16,131,128]{2,1,0:T(8,128)}, u32[]{:S(2)}, u32[]{:S(2)}) async-start(f32[16,131,128]{2,1,0:T(8,128)} %broadcast_in_dim.85), calls=%async_computation.2 | async-start | bytes 2228224 | tf_op jit(solution)/shard_map/all_to_all | solution.py:268
  154.3 34.4 %copy-start.27 = (f32[1,256,16]{1,2,0:T(8,128)S(1)}, f32[1,256,16]{1,2,0:T(8,128)}, u32[]{:S(2)}) copy-start(f32[1,256,16]{1,2,0:T(8,128)} %copy.433) | copy-start | bytes 49156
  193.6 7.8 %copy-start.5 = (f32[512,256]{1,0:T(8,128)S(1)}, f32[512,256]{1,0:T(8,128)}, u32[]{:S(2)}) copy-start(f32[512,256]{1,0:T(8,128)} %copy-done.4) | copy-start | bytes 1572868
  193.6 7.8 %copy-start.33 = (f32[1,256,16]{1,2,0:T(8,128)S(1)}, f32[1,256,16]{1,2,0:T(8,128)}, u32[]{:S(2)}) copy-start(f32[1,256,16]{1,2,0:T(8,128)} %copy.434) | copy-start | bytes 49156
  (34 other events, 143.8 us)

commit v4 on v2

--- a/solution.py
+++ b/solution.py
@@ -90,18 +90,24 @@
     return (renewed, intra_span + carried)
 
 
-def decode_mamba(ssm_state, heads_x, heads_b, heads_c, step_dt, rates, gains):
-    decays = jnp.exp(-step_dt * rates)
-    from_prefix = jnp.einsum("jrhn,hpn->jrhp", heads_c, ssm_state, precision=HIGH)
+def decode_mamba(ssm_state, heads_x, group_b, group_c, step_dt, rates, gains):
+    steps, rows, group_count, heads_each, width = heads_x.shape
+    shaped = lambda value: value.reshape(steps, rows, group_count, heads_each)
+    decays = shaped(jnp.exp(-step_dt * rates))
+    step_dt = shaped(step_dt)
+    gains = gains.reshape(group_count, heads_each)
+    grouped_state = ssm_state.reshape(group_count, heads_each, width, -1)
+    from_prefix = jnp.einsum("jrgn,gepn->jrgep", group_c, grouped_state, precision=HIGH)
     results = []
-    for current in range(heads_x.shape[0]):
+    for current in range(steps):
         factor = jnp.ones(decays.shape[1:], jnp.float32)
-        accumulated = gains[None, :, None] * heads_x[current]
+        accumulated = gains[None, :, :, None] * heads_x[current]
         for earlier in range(current, -1, -1):
-            intersection = jnp.sum(heads_c[current] * heads_b[earlier], axis=-1)
+            intersection = jnp.sum(group_c[current] * group_b[earlier], axis=-1)
             accumulated = (
                 accumulated
-                + (factor * step_dt[earlier] * intersection)[..., None] * heads_x[earlier]
+                + (factor * step_dt[earlier] * intersection[..., None])[..., None]
+                * heads_x[earlier]
             )
             factor = factor * decays[earlier]
         accumulated = accumulated + factor[..., None] * from_prefix[current]
@@ -307,12 +313,12 @@
         ),
         kernel_dc,
     )
-    heads_x = step_x.reshape(STEPS, rows_here, state_heads, HDIM)
-    heads_b = jnp.repeat(step_b.reshape(STEPS, rows_here, dgroup_count, STATE), dheads_each, axis=2)
-    heads_c = jnp.repeat(step_c.reshape(STEPS, rows_here, dgroup_count, STATE), dheads_each, axis=2)
+    heads_x = step_x.reshape(STEPS, rows_here, dgroup_count, dheads_each, HDIM)
+    group_b = step_b.reshape(STEPS, rows_here, dgroup_count, STATE)
+    group_c = step_c.reshape(STEPS, rows_here, dgroup_count, STATE)
     dec_rates = lax.dynamic_slice_in_dim(decay_rate, dec_begin, state_heads, 0)
     dec_gains = lax.dynamic_slice_in_dim(skip_gain, dec_begin, state_heads, 0)
-    mamba_out = decode_mamba(prefix_state, heads_x, heads_b, heads_c, dec_dt, dec_rates, dec_gains)
+    mamba_out = decode_mamba(prefix_state, heads_x, group_b, group_c, dec_dt, dec_rates, dec_gains)
     dec_y = mamba_out.reshape(STEPS, rows_here, state_heads * HDIM).astype(jnp.bfloat16)
 
     head_start = seq_index * own_heads

time: 225 us -> 226 us (level)
    dot_general x0 -> x1, matrix products: none -> 2.56 us  [decode_mamba(): jnp.einsum('jrgn,gepn->jrgep', group_c, grouped_state, precision=HIGH)]
    another operation x10 -> x9, other arithmetic: 4.55 us -> 4.55 us
where the time goes in v4:
time: 226 us; the launch traced here: 221 us
  local copies, waits for them, and re-layouts  58.5 us (26%)
  starting transfers between devices  52.5 us (23%)
  other arithmetic  38.2 us (17%)
  waiting for transfers between devices  37.1 us (16%)
  matrix products  33.2 us (15%)
    all_to_all x1, waiting for transfers between devices, on_device(): lax.all_to_all(copies, 'grp', 0, 0, tiled=False).reshape(grp_count, -1)  21.1 us
    all_to_all x1, starting transfers between devices, on_device(): lax.all_to_all(copies, 'grp', 0, 0, tiled=False).reshape(grp_count, -1)  18.2 us
    all_to_all x2, starting transfers between devices, exchanged(): arrived = lax.all_to_all(packed, axis, 0, 0, tiled=False)  16 us
    unnamed x124, local copies, waits for them, and re-layouts  13.6 us
    all_to_all x2, waiting for transfers between devices, exchanged(): arrived = lax.all_to_all(packed, axis, 0, 0, tiled=False)  12.3 us
    dot_general x2, matrix products, span_pass(): jnp.einsum('kts,skp->tkp', weights * intersection[None], inputs, precisio...  11.5 us
    ppermute x3, starting transfers between devices, passed_along(): lax.ppermute(value, axis, [(source, source + steps) for source in range(f...  10.1 us
    all_to_all x1, starting transfers between devices, on_device(): returned = lax.all_to_all(entering, 'seq', 0, 0, tiled=False)  6.2 us
  transfers between devices with their start and end apart: 8, of which 4 were waited for; matrix products, arithmetic and copies ran while one was open for 41% of the time, Pallas kernels for 0%

profile of v4, /device:TPU:8, one launch (start us, length us, event | category | flops | bytes accessed | tf_op | source)
XLA Modules:
  0.0 221.2 jit_solution(10823773433285125395)
XLA Ops:
  1.5 3.5 %collective-permute-start = (f32[3,1024]{1,0:T(4,128)S(1)}, f32[3,1024]{1,0:T(4,128)S(1)}, u32[]{:S(2)}, u32[]{:S(2)}) collective-permute-start(f32[3,1024]{1,0:T(4,128)S(1)} %slice.460), channel_id=1, source_target_pairs={{0,16},{16,32},{32,48},{48,64},{64,80},{80,96},{96,112},{112,128},... | collective-permute-start | bytes 36872 | tf_op jit(solution)/shard_map/ppermute | solution.py:48
  6.0 3.2 %collective-permute-start.2 = (f32[3,256]{1,0:T(4,128)S(1)}, f32[3,256]{1,0:T(4,128)S(1)}, u32[]{:S(2)}, u32[]{:S(2)}) collective-permute-start(f32[3,256]{1,0:T(4,128)S(1)} %slice.474), channel_id=1, source_target_pairs={{0,16},{16,32},{32,48},{48,64},{64,80},{80,96},{96,112},{112,128},... | collective-permute-start | bytes 9224 | tf_op jit(solution)/shard_map/ppermute | solution.py:48
  11.6 3.5 %collective-permute-start.1 = (f32[3,256]{1,0:T(4,128)}, f32[3,256]{1,0:T(4,128)}, u32[]{:S(2)}, u32[]{:S(2)}) collective-permute-start(f32[3,256]{1,0:T(4,128)} %slice.468), channel_id=1, source_target_pairs={{0,16},{16,32},{32,48},{48,64},{64,80},{80,96},{96,112},{112,128},... | collective-permute-start | bytes 9224 | tf_op jit(solution)/shard_map/ppermute | solution.py:48
  30.1 4.6 %divide_multiply_fusion = f32[512,1024]{1,0:T(8,128)S(1)} fusion(f32[512,1024]{1,0:T(8,128)} %convert_element_type.44, f32[3,1024]{1,0:T(4,128)S(1)} %collective-permute-done, f32[1024]{0:T(1024)S(1)} %bitcast.420, f32[1024]{0:T(1024)S(1)} %bitcast.418, f32[1024]{0:T(1024)S(1)} %bitcast.419, f32[1024]{0:T(1024)S(1)} %bitcast.417), kind=kLoop, calls=%fused_computation.33 | loop fusion | flops 7340032 | bytes 4222976 | tf_op jit(solution)/shard_map/jit(silu)/mul | solution.py:57
  41.8 2.3 %reshape.1490 = f32[16,128,128]{2,1,0:T(8,128)} reshape(f32[16,64,256]{2,1,0:T(8,128)} %convolution_add_fusion) | data formatting | bytes 2097152 | tf_op jit(solution)/shard_map/reshape | solution.py:31
  44.1 2.3 %pad_maximum_fusion.1 = f32[16,132,128]{2,1,0:T(8,128)} fusion(f32[16,1,128]{2,1,0:T(1,128)S(1)} %bitcast.410, f32[16,2,128]{2,1,0:T(2,128)S(1)} %reshape.1494, f32[16,1,128]{2,1,0:T(1,128)S(1)} %bitcast.409, f32[16,128,128]{2,1,0:T(8,128)} %reshape.1490), kind=kLoop, calls=%fused_computation.57 | loop fusion | flops 811008 | bytes 2162688 | tf_op jit(solution)/shard_map/concatenate | solution.py:29
  46.4 7.8 %all-to-all-start = ((f32[16,132,128]{2,1,0:T(8,128)}), f32[16,132,128]{2,1,0:T(8,128)}, u32[]{:S(2)}, u32[]{:S(2)}) async-start(f32[16,132,128]{2,1,0:T(8,128)} %pad_maximum_fusion.1), calls=%async_computation | async-start | bytes 2228224 | tf_op jit(solution)/shard_map/all_to_all | solution.py:36
  54.1 3.1 %fusion.157 = (bf16[1,8,64,1024]{3,2,1,0:T(8,128)(2,1)}, bf16[1,8,64,1024]{3,2,1,0:T(8,128)(2,1)}) fusion(bf16[2,8,64,1024]{3,2,1,0:T(8,128)(2,1)} %param.28), kind=kLoop, calls=%fused_computation.281 | loop fusion | bytes 4194304 | tf_op jit(solution)/shard_map/slice | solution.py:204
  71.8 5.7 %all-to-all-done = f32[16,132,128]{2,1,0:T(8,128)} async-done(((f32[16,132,128]{2,1,0:T(8,128)}), f32[16,132,128]{2,1,0:T(8,128)}, u32[]{:S(2)}, u32[]{:S(2)}) %all-to-all-start) | async-done | bytes 1081376 | tf_op jit(solution)/shard_map/all_to_all | solution.py:36
  77.5 8.2 %all-to-all-start.3 = ((f32[16,66,128]{2,1,0:T(8,128)}), f32[16,66,128]{2,1,0:T(8,128)}, u32[]{:S(2)}, u32[]{:S(2)}) async-start(f32[16,66,128]{2,1,0:T(8,128)} %copy.328), calls=%async_computation.3 | async-start | bytes 1179648 | tf_op jit(solution)/shard_map/all_to_all | solution.py:36
  93.4 6.6 %all-to-all-done.3 = f32[16,66,128]{2,1,0:T(8,128)} async-done(((f32[16,66,128]{2,1,0:T(8,128)}), f32[16,66,128]{2,1,0:T(8,128)}, u32[]{:S(2)}, u32[]{:S(2)}) %all-to-all-start.3) | async-done | bytes 540704 | tf_op jit(solution)/shard_map/all_to_all | solution.py:36
  100.0 6.2 %all-to-all-start.1 = ((f32[16,128,128]{2,1,0:T(8,128)}), f32[16,128,128]{2,1,0:T(8,128)}, u32[]{:S(2)}, u32[]{:S(2)}) async-start(f32[16,128,128]{2,1,0:T(8,128)} %copy.305), calls=%async_computation.1 | async-start | bytes 2097152 | tf_op jit(solution)/shard_map/all_to_all | solution.py:251
  124.4 3.7 %collective-permute-done.3 = f32[131,128]{1,0:T(8,128)S(1)} collective-permute-done((f32[131,128]{1,0:T(8,128)S(1)}, f32[131,128]{1,0:T(8,128)S(1)}, u32[]{:S(2)}, u32[]{:S(2)}) %collective-permute-start.3) | collective-permute-done | bytes 67104 | tf_op jit(solution)/shard_map/ppermute | solution.py:263
  129.2 18.2 %all-to-all-start.2 = ((f32[16,131,128]{2,1,0:T(8,128)}), f32[16,131,128]{2,1,0:T(8,128)}, u32[]{:S(2)}, u32[]{:S(2)}) async-start(f32[16,131,128]{2,1,0:T(8,128)} %broadcast_in_dim.85), calls=%async_computation.2 | async-start | bytes 2228224 | tf_op jit(solution)/shard_map/all_to_all | solution.py:265
  154.9 2.5 %reshape.1499 = f32[16,64,256]{2,1,0:T(8,128)} reshape(f32[16,128,128]{2,1,0:T(8,128)} %all-to-all-done.1) | data formatting | bytes 2097152 | tf_op jit(solution)/shard_map/reshape.111
  157.4 21.1 %all-to-all-done.2 = f32[16,131,128]{2,1,0:T(8,128)} async-done(((f32[16,131,128]{2,1,0:T(8,128)}), f32[16,131,128]{2,1,0:T(8,128)}, u32[]{:S(2)}, u32[]{:S(2)}) %all-to-all-start.2) | async-done | bytes 1073184 | tf_op jit(solution)/shard_map/all_to_all | solution.py:265
  183.0 2.3 %slice.514 = f32[16,16384]{1,0:T(8,128)} slice(f32[16,16768]{1,0:T(8,128)} %bitcast.371), slice={[0:16], [0:16384]} | slice | bytes 2097152 | tf_op jit(solution)/shard_map/slice | solution.py:267
  191.3 2.6 %copy.366 = f32[2,8,64,256]{3,2,1,0:T(8,128)} copy(f32[2,8,64,256]{3,1,2,0:T(8,128)} %bitcast.372) | data formatting | bytes 2097152
  195.5 2.6 %convolution_bitcast_fusion.2 = f32[2,8,1,16,64]{4,1,0,3,2:T(8,128)S(1)} fusion(f32[16,64,256,1]{2,1,0,3:T(8,128)} %bitcast.373, f32[1,8,256]{2,1,0:T(8,128)S(1)} %divide_multiply_fusion.4, f32[1,8,256]{2,1,0:T(8,128)S(1)} %get-tuple-element.19), kind=kOutput, calls=%fused_computation.53 | convolution fusion | flops 50335744 | bytes 1130496 | tf_op jit(solution)/shard_map/jrgn,gepn->jrgep/dot_general | solution.py:100
  199.7 6.5 %fusion.41 = f32[256,16,64]{0,2,1:T(8,128)S(1)} fusion(f32[1,256,16,64]{1,3,2,0:T(8,128)} %fusion.36, f32[256,256]{1,0:T(8,128)S(1)} %copy-done.16, f32[16,256]{1,0:T(8,128)S(1)} %copy-done.44, pred[256,256]{1,0:T(8,128)(4,1)S(1)} %copy-done.36, f32[1,512,16,64]{1,3,2,0:T(8,128)} %copy-done.1), kind=kOutput, calls=%fused_computation.46 | convolution fusion | flops 809762816 | bytes 3506176 | tf_op jit(solution)/shard_map/vmap(kts,skp->tkp)/dot_general | solution.py:83
  206.2 5.0 %fusion.47 = f32[256,16,64]{0,2,1:T(8,128)S(1)} fusion(f32[1,256,16,64]{1,3,2,0:T(8,128)S(1)} %fusion.37, f32[256,256]{1,0:T(8,128)S(1)} %copy-done.15, f32[16,256]{1,0:T(8,128)S(1)} %copy-done.45, pred[256,256]{1,0:T(8,128)(4,1)S(1)} %copy-done.36, f32[1,512,16,64]{1,3,2,0:T(8,128)S(1)} %copy-done.2), kind=kOutput, calls=%fused_computation.48 | convolution fusion | flops 809762816 | bytes 3506176 | tf_op jit(solution)/shard_map/vmap(kts,skp->tkp)/dot_general | solution.py:83
  211.2 3.3 %maximum_add_fusion = f32[512,16,64]{0,2,1:T(8,128)} fusion(f32[256,16,64]{0,2,1:T(8,128)S(1)} %fusion.41, f32[256,16,64]{0,2,1:T(8,128)S(1)} %fusion.47, f32[16,64,256]{2,1,0:T(8,128)S(1)} %copy-done.9, f32[512,16]{0,1:T(8,128)S(1)} %bitcast.388, f32[512,256]{1,0:T(8,128)S(1)} %copy-done.4), kind=kOutput, calls=%fused_computation.23 | convolution fusion | flops 1612185600 | bytes 5799936 | tf_op jit(solution)/shard_map/gsn,gkpn->gskp/dot_general | solution.py:283
  214.6 2.9 %copy.306 = f32[512,1024]{1,0:T(8,128)} copy(f32[512,1024]{0,1:T(8,128)} %bitcast.364) | data formatting | bytes 4194304 | tf_op jit(solution)/shard_map/reshape;transpose | solution.py:287
  218.1 3.1 %add_convert_fusion = bf16[512,1024]{1,0:T(8,128)(2,1)} fusion(f32[512,1024]{1,0:T(8,128)} %copy.306, f32[512,1024]{1,0:T(8,128)S(1)} %divide_multiply_fusion, f32[1024]{0:T(1024)S(1)} %copy-done.46), kind=kLoop, calls=%fused_computation.24 | loop fusion | flops 1572864 | bytes 5246976 | tf_op jit(solution)/shard_map/convert_element_type | solution.py:290
  (289 shorter events, 88.9 us)
Async XLA Ops:
  0.6 59.6 %copy-start = (bf16[2,8,8192]{2,1,0:T(8,128)(2,1)S(1)}, bf16[2,8,8192]{2,1,0:T(8,128)(2,1)}, u32[]{:S(2)}) copy-start(bf16[2,8,8192]{2,1,0:T(8,128)(2,1)} %param.26) | copy-start | bytes 786436
  0.6 26.5 %copy-start.13 = (bf16[512,1024]{1,0:T(8,128)(2,1)S(1)}, bf16[512,1024]{1,0:T(8,128)(2,1)}, u32[]{:S(2)}) copy-start(bf16[512,1024]{1,0:T(8,128)(2,1)} %param.15) | copy-start | bytes 3145732
  1.5 28.7 %collective-permute-start = (f32[3,1024]{1,0:T(4,128)S(1)}, f32[3,1024]{1,0:T(4,128)S(1)}, u32[]{:S(2)}, u32[]{:S(2)}) collective-permute-start(f32[3,1024]{1,0:T(4,128)S(1)} %slice.460), channel_id=1, source_target_pairs={{0,16},{16,32},{32,48},{48,64},{64,80},{80,96},{96,112},{112,128},... | collective-permute-start | bytes 36872 | tf_op jit(solution)/shard_map/ppermute | solution.py:48
  6.0 23.0 %collective-permute-start.2 = (f32[3,256]{1,0:T(4,128)S(1)}, f32[3,256]{1,0:T(4,128)S(1)}, u32[]{:S(2)}, u32[]{:S(2)}) collective-permute-start(f32[3,256]{1,0:T(4,128)S(1)} %slice.474), channel_id=1, source_target_pairs={{0,16},{16,32},{32,48},{48,64},{64,80},{80,96},{96,112},{112,128},... | collective-permute-start | bytes 9224 | tf_op jit(solution)/shard_map/ppermute | solution.py:48
  11.6 173.7 %collective-permute-start.1 = (f32[3,256]{1,0:T(4,128)}, f32[3,256]{1,0:T(4,128)}, u32[]{:S(2)}, u32[]{:S(2)}) collective-permute-start(f32[3,256]{1,0:T(4,128)} %slice.468), channel_id=1, source_target_pairs={{0,16},{16,32},{32,48},{48,64},{64,80},{80,96},{96,112},{112,128},... | collective-permute-start | bytes 9224 | tf_op jit(solution)/shard_map/ppermute | solution.py:48
  46.4 31.1 %all-to-all-start = ((f32[16,132,128]{2,1,0:T(8,128)}), f32[16,132,128]{2,1,0:T(8,128)}, u32[]{:S(2)}, u32[]{:S(2)}) async-start(f32[16,132,128]{2,1,0:T(8,128)} %pad_maximum_fusion.1), calls=%async_computation | async-start | bytes 2228224 | tf_op jit(solution)/shard_map/all_to_all | solution.py:36
  77.5 22.5 %all-to-all-start.3 = ((f32[16,66,128]{2,1,0:T(8,128)}), f32[16,66,128]{2,1,0:T(8,128)}, u32[]{:S(2)}, u32[]{:S(2)}) async-start(f32[16,66,128]{2,1,0:T(8,128)} %copy.328), calls=%async_computation.3 | async-start | bytes 1179648 | tf_op jit(solution)/shard_map/all_to_all | solution.py:36
  92.0 14.2 %copy-start.42 = (f32[2,8,16]{2,1,0:T(8,128)S(1)}, f32[2,8,16]{2,1,0:T(8,128)}, u32[]{:S(2)}) copy-start(f32[2,8,16]{2,1,0:T(8,128)} %param.25) | copy-start | bytes 3076
  92.0 14.2 %copy-start.51 = (f32[16]{0:T(128)S(1)}, f32[16]{0:T(128)}, u32[]{:S(2)}) copy-start(f32[16]{0:T(128)} %get-tuple-element.78) | copy-start | bytes 196
  92.0 14.8 %copy-start.20 = (f32[1,16,2,128]{3,1,2,0:T(8,128)S(1)}, f32[1,16,2,128]{3,1,2,0:T(8,128)}, u32[]{:S(2)}) copy-start(f32[1,16,2,128]{3,1,2,0:T(8,128)} %copy-done.19) | copy-start | bytes 49156
  92.0 16.1 %copy-start.50 = (f32[16]{0:T(128)S(1)}, f32[16]{0:T(128)}, u32[]{:S(2)}) copy-start(f32[16]{0:T(128)} %get-tuple-element.72) | copy-start | bytes 196
  92.1 16.8 %copy-start.30 = (f32[16,4,128]{2,0,1:T(8,128)S(1)}, f32[16,4,128]{2,0,1:T(8,128)}, u32[]{:S(2)}) copy-start(f32[16,4,128]{2,0,1:T(8,128)} %get-tuple-element.59) | copy-start | bytes 98308
  92.1 18.7 %copy-start.37 = (f32[1,256,16]{1,0,2:T(1,128)S(1)}, f32[1,256,16]{1,0,2:T(1,128)}, u32[]{:S(2)}) copy-start(f32[1,256,16]{1,0,2:T(1,128)} %get-tuple-element.24) | copy-start | bytes 49156
  92.1 19.3 %copy-start.31 = (bf16[2,8,1024]{2,1,0:T(8,128)(2,1)S(1)}, bf16[2,8,1024]{2,1,0:T(8,128)(2,1)}, u32[]{:S(2)}) copy-start(bf16[2,8,1024]{2,1,0:T(8,128)(2,1)} %param.22) | copy-start | bytes 98308
  100.0 28.1 %all-to-all-start.1 = ((f32[16,128,128]{2,1,0:T(8,128)}), f32[16,128,128]{2,1,0:T(8,128)}, u32[]{:S(2)}, u32[]{:S(2)}) async-start(f32[16,128,128]{2,1,0:T(8,128)} %copy.305), calls=%async_computation.1 | async-start | bytes 2097152 | tf_op jit(solution)/shard_map/all_to_all | solution.py:251
  122.3 25.1 %copy-start.25 = (f32[16,2,128]{2,1,0:T(2,128)S(1)}, f32[16,2,128]{2,1,0:T(2,128)}, u32[]{:S(2)}) copy-start(f32[16,2,128]{2,1,0:T(2,128)} %copy-done.24) | copy-start | bytes 49156
  122.3 25.7 %copy-start.32 = (bf16[2,8,8,128]{3,1,2,0:T(8,128)(2,1)S(1)}, bf16[2,8,8,128]{3,1,2,0:T(8,128)(2,1)}, u32[]{:S(2)}) copy-start(bf16[2,8,8,128]{3,1,2,0:T(8,128)(2,1)} %get-tuple-element.57) | copy-start | bytes 98308
  122.3 28.3 %copy-start.23 = (f32[2,8,64,2]{2,1,3,0:T(8,128)S(1)}, f32[2,8,64,2]{2,1,3,0:T(8,128)}, u32[]{:S(2)}) copy-start(f32[2,8,64,2]{2,1,3,0:T(8,128)} %copy-done.22) | copy-start | bytes 24580
  122.4 5.8 %collective-permute-start.3 = (f32[131,128]{1,0:T(8,128)S(1)}, f32[131,128]{1,0:T(8,128)S(1)}, u32[]{:S(2)}, u32[]{:S(2)}) collective-permute-start(f32[131,128]{1,0:T(8,128)S(1)} %pad_bitcast_fusion), channel_id=1, source_target_pairs={{0,0},{1,16},{2,32},{3,48},{4,64},{5,80},{6,96},{7,112},{8,128},{9... | collective-permute-start | bytes 201224 | tf_op jit(solution)/shard_map/ppermute | solution.py:263
  129.2 18.2 %copy-start.35 = (f32[1,16,2,128]{3,2,1,0:T(2,128)S(1)}, f32[1,16,2,128]{3,2,1,0:T(2,128)}, u32[]{:S(2)}) copy-start(f32[1,16,2,128]{3,2,1,0:T(2,128)} %copy.292) | copy-start | bytes 49156
  129.2 49.3 %all-to-all-start.2 = ((f32[16,131,128]{2,1,0:T(8,128)}), f32[16,131,128]{2,1,0:T(8,128)}, u32[]{:S(2)}, u32[]{:S(2)}) async-start(f32[16,131,128]{2,1,0:T(8,128)} %broadcast_in_dim.85), calls=%async_computation.2 | async-start | bytes 2228224 | tf_op jit(solution)/shard_map/all_to_all | solution.py:265
  190.7 7.4 %copy-start.18 = (f32[1,8,1,16,64]{4,3,1,2,0:T(8,128)S(1)}, f32[1,8,1,16,64]{4,3,1,2,0:T(8,128)}, u32[]{:S(2)}) copy-start(f32[1,8,1,16,64]{4,3,1,2,0:T(8,128)} %squeeze.67) | copy-start | bytes 98308
  190.7 7.4 %copy-start.41 = (f32[8,16]{0,1:T(8,128)S(1)}, f32[8,16]{0,1:T(8,128)}, u32[]{:S(2)}) copy-start(f32[8,16]{0,1:T(8,128)} %copy.309) | copy-start | bytes 1540
  190.7 7.4 %copy-start.49 = (f32[16]{0:T(128)S(1)}, f32[16]{0:T(128)}, u32[]{:S(2)}) copy-start(f32[16]{0:T(128)} %get-tuple-element.71) | copy-start | bytes 196
  (40 other events, 150.0 us)
